TPU v7x, 128 devices: a whole 4x4x4 slice. The times are simulated.
128 devices in a mesh: seq: 32 (over y, z, core), tp: 4 (over x).
Axes of the slice: x: 4, y: 4, z: 4, core: 2. Of those that a mesh axis runs over, the one named last changes fastest.
Arguments:
- residual: bfloat16 [8192, 3584], P(('seq', 'tp')), may hold values from -6 to 6
- x_in: bfloat16 [8192, 3584], P('seq', 'tp'), may hold values from -6 to 6
- z_in: bfloat16 [8192, 3584], P('seq', 'tp'), may hold values from -6 to 6
- bc_in: bfloat16 [8192, 128], P('seq'), may hold values from -1.5 to 1.5
- dt_in: float32 [8192, 56], P('seq', 'tp'), may hold values from -6 to 6
- conv_x_weight: float32 [4, 3584], P(None, 'tp'), may hold values from -3 to 3
- conv_bc_weight: float32 [4, 128], replicated, may hold values from -3 to 3
- conv_x_cache: bfloat16 [16, 3, 3584], P(None, None, 'tp'), may hold values from -6 to 6
- conv_bc_cache: bfloat16 [16, 3, 128], replicated, may hold values from -1.5 to 1.5
- ssm_cache: float32 [16, 56, 64, 64], P(None, 'tp'), may hold values from -12 to 12
- dt_bias: float32 [56], P('tp'), may hold values from -1 to 1
- a_log: float32 [56], P('tp'), may hold values from -9 to -3.5
- d_skip: float32 [56], P('tp'), may hold values from 0.5 to 1.5
- norm_gain: float32 [3584], P('tp'), may hold values from 0.5 to 1.5
- out_weight: bfloat16 [3584, 3584], P('tp'), may hold values from -0.09375 to 0.09375
- attn_gain: float32 [3584], replicated, may hold values from 0.5 to 1.5
- q_weight: bfloat16 [3584, 3584], P(None, 'tp'), may hold values from -1 to 1
- q_down: bfloat16 [3584, 128], replicated, may hold values from -0.09375 to 0.09375
- q_up: bfloat16 [128, 3584], P(None, 'tp'), may hold values from -0.5 to 0.5
- cache_keys: bfloat16 [8192, 3584], P('seq', 'tp'), may hold values from -6 to 6
- cache_values: bfloat16 [8192, 3584], P('seq', 'tp'), may hold values from -6 to 6
- new_keys: bfloat16 [8192, 3584], P('seq', 'tp'), may hold values from -6 to 6
- new_values: bfloat16 [8192, 3584], P('seq', 'tp'), may hold values from -6 to 6
- lengths: int32 [16], replicated, may hold values from 1 to 2304, 8192 in all
Outputs:
- hidden: bfloat16 [8192, 3584], P(('seq', 'tp'))
- attended: bfloat16 [8192, 3584], P('seq', 'tp')
Inputs may be any that keep to these rules, and one draw needn't show every extreme that they name: lengths of the prompts' second halves sum to 8192; the largest is 2304.
All inputs are finite; a program needn't handle non-finite values.
Results may differ from a plain program's by a relative error of at most 0.014.
Values may be sent and summed in bfloat16 or wider, within the bound.
No kernel may reach another device: no remote copies, remote signals or barrier semaphores. Data moves between devices by JAX's collectives and lax.ppermute only.
A program may use at most 192 MiB of HBM per device.

v0:
```python
import jax
import jax.numpy as jnp
from jax import lax
from jax.sharding import PartitionSpec as P

HA = 224


EPS = 1e-05
NEG = -1e30


def shifted_2(value, axis, steps):
    count = lax.axis_size(axis)
    initial, last = (max(0, -steps), min(count, count - steps))
    return lax.ppermute(value, axis, [(source, source + steps) for source in range(initial, last)])


def locate(lengths, index):
    ends = jnp.cumsum(lengths)
    starts = ends - lengths
    count = lengths.shape[0]
    segment = jnp.sum((index[:, None] >= ends[None, :]).astype(jnp.int32), axis=1)
    segment = jnp.minimum(segment, count - 1)
    onehot = segment[:, None] == jnp.arange(count, dtype=jnp.int32)[None, :]
    begin = jnp.sum(jnp.where(onehot, starts[None, :], 0), axis=1)
    valid = (index >= 0) & (index < ends[count - 1])
    return (segment, begin, valid, onehot)


def convolve(inputs, border, cache, weight, position, onehot):
    taps = weight.shape[0]
    length = inputs.shape[0]
    extended = jnp.concatenate([border, inputs], axis=0)
    picks = onehot.astype(jnp.bfloat16)
    cached_rows = [
        jnp.dot(picks, cache[:, slot, :], preferred_element_type=jnp.float32)
        for slot in range(taps - 1)
    ]
    result = weight[0][None, :] * inputs.astype(jnp.float32)
    for lag in range(1, taps):
        shifted = extended[taps - 1 - lag : taps - 1 - lag + length].astype(jnp.float32)
        slot_index = taps - 1 + position - lag
        fallback = jnp.zeros_like(shifted)
        for slot in range(taps - 1):
            fallback = jnp.where((slot_index == slot)[:, None], cached_rows[slot], fallback)
        shifted = jnp.where((position >= lag)[:, None], shifted, fallback)
        result = result + weight[lag][None, :] * shifted
    return jax.nn.silu(result).astype(jnp.bfloat16)


def per_device(
    residual,
    x_in,
    z_in,
    bc_in,
    dt_in,
    conv_x_weight,
    conv_bc_weight,
    conv_x_cache,
    conv_bc_cache,
    ssm_cache,
    dt_bias,
    a_log,
    d_skip,
    norm_gain,
    out_weight,
    attn_gain,
    q_weight,
    q_down,
    q_up,
    cache_keys,
    cache_values,
    new_keys,
    new_values,
    lengths,
):
    high_precision = lax.Precision.HIGH
    length = x_in.shape[0]
    taps = conv_x_weight.shape[0]
    seq_index = lax.axis_index("seq")
    seq_count = lax.axis_size("seq")
    reach = seq_count // 4 + 1
    first = seq_index * length
    local_index = first + jnp.arange(length, dtype=jnp.int32)
    segment, begin, valid, onehot = locate(lengths, local_index)
    position = local_index - begin
    x_border, bc_border = shifted_2(
        (x_in[length - taps + 1 :], bc_in[length - taps + 1 :]), "seq", 1
    )
    x_conv = convolve(x_in, x_border, conv_x_cache, conv_x_weight, position, onehot)
    bc_conv = convolve(bc_in, bc_border, conv_bc_cache, conv_bc_weight, position, onehot)
    heads = dt_bias.shape[0]
    state_size = bc_in.shape[1] // 2
    head_size = x_in.shape[1] // heads
    prompts = lengths.shape[0]
    values_bf = x_conv.reshape(length, heads, head_size)
    values = x_conv.astype(jnp.float32).reshape(length, heads, head_size)
    inputs_b = bc_conv[:, :state_size]
    inputs_c = bc_conv[:, state_size:]
    step = jax.nn.softplus(dt_in + dt_bias[None, :])
    log_decay = -step * jnp.exp(a_log)[None, :]
    cumulative = jnp.cumsum(log_decay, axis=0)
    local_begin = jnp.maximum(begin - first, 0)
    before = jnp.take(cumulative - log_decay, local_begin, axis=0)
    from_begin = jnp.exp(cumulative - before)
    block = min(length, 512)
    pair_scores = jnp.dot(inputs_c, inputs_b.T, preferred_element_type=jnp.float32)
    cumulative_t = cumulative.T
    step_t = step.T
    order = jnp.arange(length, dtype=jnp.int32)

    def intra(block_start):
        query_rows = block_start + jnp.arange(block, dtype=jnp.int32)
        same = (segment[:, None] == segment[None, :]) & (query_rows[:, None] >= order[None, :])
        gap = cumulative_t[:, :, None] - cumulative_t[:, None, :]
        factor = jnp.where(same[None], jnp.exp(jnp.where(same[None], gap, 0.0)), 0.0)
        weights = factor * step_t[:, None, :] * pair_scores[None, :, :]
        return jnp.einsum(
            "hqs,shd->qhd",
            weights,
            values_bf,
            precision=high_precision,
            preferred_element_type=jnp.float32,
        )

    intra_out = lax.map(intra, jnp.arange(length // block, dtype=jnp.int32) * block).reshape(
        length, heads, head_size
    )
    last_segment = segment[length - 1]
    in_last = segment == last_segment
    tail_weight = (
        jnp.where(in_last[:, None], jnp.exp(cumulative[length - 1][None, :] - cumulative), 0.0)
        * step
    )
    weighted = tail_weight[:, :, None] * values
    local_state = jnp.einsum(
        "thd,tn->hdn",
        weighted,
        inputs_b,
        precision=high_precision,
        preferred_element_type=jnp.float32,
    )
    whole_decay = jnp.exp(cumulative[length - 1] - before[length - 1])
    starts_here = begin[length - 1] >= first
    cached_last = lax.dynamic_index_in_dim(ssm_cache, last_segment, 0, keepdims=False)
    chain_state = local_state + jnp.where(
        starts_here, whole_decay[:, None, None] * cached_last, 0.0
    )
    chain_decay = jnp.where(starts_here, jnp.zeros_like(whole_decay), whole_decay)

    def relay(turn, incoming):
        return shifted_2(chain_decay[:, None, None] * incoming + chain_state, "seq", 1)

    carried = lax.fori_loop(0, seq_count - 1, relay, jnp.zeros_like(chain_state))
    continuing = position[0] > 0
    replace = (jnp.arange(prompts, dtype=jnp.int32) == segment[0]) & continuing
    initial = jnp.where(replace[:, None, None, None], carried[None], ssm_cache)
    selected = (onehot[:, :, None].astype(jnp.bfloat16) * inputs_c[:, None, :]).reshape(
        length, prompts * state_size
    )
    table = jnp.transpose(initial, (0, 3, 1, 2)).reshape(prompts * state_size, heads * head_size)
    init_out = (
        jnp.dot(
            selected, table, precision=high_precision, preferred_element_type=jnp.float32
        ).reshape(length, heads, head_size)
        * from_begin[:, :, None]
    )
    mixed = intra_out + init_out + d_skip[None, :, None] * values
    gated = (
        mixed * jax.nn.silu(z_in.astype(jnp.float32).reshape(length, heads, head_size))
    ).reshape(length, heads * head_size)
    squares = lax.psum(jnp.sum(gated * gated, axis=1), "tp")
    width = gated.shape[1] * lax.axis_size("tp")
    normed = (gated * lax.rsqrt(squares / width + EPS)[:, None] * norm_gain[None, :]).astype(
        jnp.bfloat16
    )
    summed = lax.psum_scatter(
        jnp.dot(normed, out_weight, preferred_element_type=jnp.float32),
        "tp",
        scatter_dimension=0,
        tiled=True,
    )
    hidden = (residual.astype(jnp.float32) + summed).astype(jnp.bfloat16)
    level = hidden.astype(jnp.float32)
    attn_in = (
        level * lax.rsqrt(jnp.mean(level * level, axis=1, keepdims=True) + EPS) * attn_gain[None, :]
    ).astype(jnp.bfloat16)
    piece = lax.all_gather(attn_in, "tp", axis=0, tiled=True)
    low = jnp.dot(piece, q_down, preferred_element_type=jnp.float32).astype(jnp.bfloat16)
    query = (
        jnp.dot(piece, q_weight, preferred_element_type=jnp.float32)
        + jnp.dot(low, q_up, preferred_element_type=jnp.float32)
    ).astype(jnp.bfloat16)
    count_heads = query.shape[1] // HA

    def piece_mask(query_index, query_segment, offset, causal):
        key_index = (seq_index + offset) * length + jnp.arange(length, dtype=jnp.int32)
        key_segment, _, key_valid, _ = locate(lengths, key_index)
        allowed = key_valid[None, :] & (key_segment[None, :] == query_segment[:, None])
        if causal:
            allowed = allowed & (key_index[None, :] <= query_index[:, None])
        return allowed

    cache_pieces = [(cache_keys, cache_values, 0)]
    new_pieces = [(new_keys, new_values, 0)]
    for distance in range(1, reach + 1):
        behind = shifted_2((cache_keys, cache_values, new_keys, new_values), "seq", distance)
        cache_pieces.append((behind[0], behind[1], -distance))
        new_pieces.append((behind[2], behind[3], -distance))
        forward = shifted_2((cache_keys, cache_values), "seq", -distance)
        cache_pieces.append((forward[0], forward[1], distance))
    all_keys = jnp.concatenate(
        [entry[0] for entry in cache_pieces] + [entry[0] for entry in new_pieces], axis=0
    )
    all_values = jnp.concatenate(
        [entry[1] for entry in cache_pieces] + [entry[1] for entry in new_pieces], axis=0
    )
    mask = jnp.concatenate(
        [piece_mask(local_index, segment, entry[2], False) for entry in cache_pieces]
        + [piece_mask(local_index, segment, entry[2], True) for entry in new_pieces],
        axis=1,
    )
    scale = 1.0 / HA**0.5

    def attend(head):
        column = head * HA
        query_head = lax.dynamic_slice_in_dim(query, column, HA, 1)
        key_head = lax.dynamic_slice_in_dim(all_keys, column, HA, 1)
        value_head = lax.dynamic_slice_in_dim(all_values, column, HA, 1)
        scores = (
            lax.dot_general(
                query_head, key_head, (((1,), (1,)), ((), ())), preferred_element_type=jnp.float32
            )
            * scale
        )
        scores = jnp.where(mask, scores, NEG)
        top = jnp.max(scores, axis=1, keepdims=True)
        weights = jnp.exp(scores - top)
        probs = (weights / jnp.sum(weights, axis=1, keepdims=True)).astype(jnp.bfloat16)
        return jnp.dot(probs, value_head, preferred_element_type=jnp.float32).astype(jnp.bfloat16)

    per_head = lax.map(attend, jnp.arange(count_heads, dtype=jnp.int32))
    attended = jnp.transpose(per_head, (1, 0, 2)).reshape(length, count_heads * HA)
    return (hidden, attended)


def solution(mesh):
    in_specs = (
        P(("seq", "tp"), None),
        P("seq", "tp"),
        P("seq", "tp"),
        P("seq", None),
        P("seq", "tp"),
        P(None, "tp"),
        P(),
        P(None, None, "tp"),
        P(),
        P(None, "tp", None, None),
        P("tp"),
        P("tp"),
        P("tp"),
        P("tp"),
        P("tp", None),
        P(),
        P(None, "tp"),
        P(),
        P(None, "tp"),
        P("seq", "tp"),
        P("seq", "tp"),
        P("seq", "tp"),
        P("seq", "tp"),
        P(),
    )
    out_specs = (P(("seq", "tp"), None), P("seq", "tp"))
    return jax.shard_map(
        per_device, mesh=mesh, in_specs=in_specs, out_specs=out_specs, check_vma=False
    )
```

profile of v0, /device:TPU:16, one launch (start us, length us, event | category | flops | bytes accessed | tf_op | source)
XLA Modules:
  0.0 1018.3 jit_solution(5846869598163755557)
XLA Ops:
  78.7 372.7 %while.24 = (s32[]{:T(128)}, f32[14,64,64]{2,1,0:T(8,128)S(1)}, f32[14]{0:T(128)S(1)}, f32[14,64,64]{2,1,0:T(8,128)S(1)}, s32[]{:T(128)}) while((s32[]{:T(128)}, f32[14,64,64]{2,1,0:T(8,128)S(1)}, f32[14]{0:T(128)S(1)}, f32[14,64,64]{2,1,0:T(8,128)S(1)}, s32[]{:T(128)}) %tuple.107), condition=%wide.region_6.7_spmd, body=%wide.region_5.6_spmd.sunk | while | flops 114690 | bytes 1605789 | solution.py:155
  80.7 10.0 collective-permute-done
  92.8 10.0 collective-permute-done
  104.8 10.0 collective-permute-done
  116.8 10.0 collective-permute-done
  128.8 10.0 collective-permute-done
  140.9 10.0 collective-permute-done
  152.9 10.0 collective-permute-done
  164.9 10.0 collective-permute-done
  176.9 10.0 collective-permute-done
  188.9 10.0 collective-permute-done
  201.0 10.0 collective-permute-done
  213.0 10.0 collective-permute-done
  225.0 10.0 collective-permute-done
  237.0 10.0 collective-permute-done
  249.0 10.0 collective-permute-done
  261.1 10.0 collective-permute-done
  309.2 10.0 collective-permute-done
  321.2 10.0 collective-permute-done
  333.2 10.0 collective-permute-done
  477.8 10.6 %psum.7 = f32[256]{0:T(256)S(1)} all-reduce(f32[256]{0:T(256)S(1)} %get-tuple-element.175), channel_id=1, replica_groups=mesh['seq'=32,'tp'=4] {'tp'}, use_global_device_ids=true, to_apply=%region_8.9 | all-reduce | flops 256 | bytes 2048 | tf_op jit(solution)/shard_map/psum | solution.py:173
  549.1 12.0 %collective-permute-done.8 = bf16[256,896]{1,0:T(8,128)(2,1)S(1)} collective-permute-done((bf16[256,896]{1,0:T(8,128)(2,1)}, bf16[256,896]{1,0:T(8,128)(2,1)S(1)}, u32[]{:S(2)}, u32[]{:S(2)}) %collective-permute-start.8) | collective-permute-done | bytes 458784 | tf_op jit(solution)/shard_map/ppermute | solution.py:16
  563.8 18.2 %collective-permute-start.14 = (bf16[256,896]{1,0:T(8,128)(2,1)}, bf16[256,896]{1,0:T(8,128)(2,1)S(1)}, u32[]{:S(2)}, u32[]{:S(2)}) collective-permute-start(bf16[256,896]{1,0:T(8,128)(2,1)} %param.47), channel_id=1, source_target_pairs={{24,0},{28,4},{32,8},{36,12},{40,16},{44,20},{48,24},{52,28},{56,3... | collective-permute-start | bytes 1376264 | tf_op jit(solution)/shard_map/ppermute | solution.py:16
  658.6 16.2 %collective-permute-done.35 = bf16[256,896]{1,0:T(8,128)(2,1)S(1)} collective-permute-done((bf16[256,896]{1,0:T(8,128)(2,1)S(1)}, bf16[256,896]{1,0:T(8,128)(2,1)S(1)}, u32[]{:S(2)}, u32[]{:S(2)}) %collective-permute-start.35) | collective-permute-done | bytes 458784 | tf_op jit(solution)/shard_map/ppermute | solution.py:16
  677.6 10.9 %collective-permute-start.40 = (bf16[256,896]{1,0:T(8,128)(2,1)S(1)}, bf16[256,896]{1,0:T(8,128)(2,1)S(1)}, u32[]{:S(2)}, u32[]{:S(2)}) collective-permute-start(bf16[256,896]{1,0:T(8,128)(2,1)S(1)} %copy-done.4), channel_id=1, source_target_pairs={{0,24},{4,28},{8,32},{12,36},{16,40},{20,44},{24,48},{28,52},{32,5... | collective-permute-start | bytes 1376264 | tf_op jit(solution)/shard_map/ppermute | solution.py:16
  689.3 16.0 %collective-permute-start.41 = (bf16[256,896]{1,0:T(8,128)(2,1)S(1)}, bf16[256,896]{1,0:T(8,128)(2,1)S(1)}, u32[]{:S(2)}, u32[]{:S(2)}) collective-permute-start(bf16[256,896]{1,0:T(8,128)(2,1)S(1)} %copy-done.4), channel_id=1, source_target_pairs={{24,0},{28,4},{32,8},{36,12},{40,16},{44,20},{48,24},{52,28},{56,3... | collective-permute-start | bytes 1376264 | tf_op jit(solution)/shard_map/ppermute | solution.py:16
  788.0 11.2 %collective-permute-start.49 = (bf16[256,896]{1,0:T(8,128)(2,1)}, bf16[256,896]{1,0:T(8,128)(2,1)S(1)}, u32[]{:S(2)}, u32[]{:S(2)}) collective-permute-start(bf16[256,896]{1,0:T(8,128)(2,1)} %param.50), channel_id=1, source_target_pairs={{0,8},{4,12},{8,16},{12,20},{16,24},{20,28},{24,32},{28,36},{32,40... | collective-permute-start | bytes 1376264 | tf_op jit(solution)/shard_map/ppermute | solution.py:16
  809.2 10.2 collective-permute-start.51
  836.1 17.0 %collective-permute-done.49 = bf16[256,896]{1,0:T(8,128)(2,1)S(1)} collective-permute-done((bf16[256,896]{1,0:T(8,128)(2,1)}, bf16[256,896]{1,0:T(8,128)(2,1)S(1)}, u32[]{:S(2)}, u32[]{:S(2)}) %collective-permute-start.49) | collective-permute-done | bytes 458784 | tf_op jit(solution)/shard_map/ppermute | solution.py:16
  866.7 12.8 %collective-permute-done.54 = bf16[256,896]{1,0:T(8,128)(2,1)S(1)} collective-permute-done((bf16[256,896]{1,0:T(8,128)(2,1)S(1)}, bf16[256,896]{1,0:T(8,128)(2,1)S(1)}, u32[]{:S(2)}, u32[]{:S(2)}) %collective-permute-start.54) | collective-permute-done | bytes 458784 | tf_op jit(solution)/shard_map/ppermute | solution.py:16
  881.1 61.9 %collective-permute-done.56 = bf16[256,896]{1,0:T(8,128)(2,1)S(1)} collective-permute-done((bf16[256,896]{1,0:T(8,128)(2,1)S(1)}, bf16[256,896]{1,0:T(8,128)(2,1)S(1)}, u32[]{:S(2)}, u32[]{:S(2)}) %collective-permute-start.56) | collective-permute-done | bytes 458784 | tf_op jit(solution)/shard_map/ppermute | solution.py:16
  952.9 56.2 %while.25 = (s32[]{:T(128)}, bf16[4,256,224]{1,2,0:T(8,128)(2,1)}, s32[4]{0:T(128)S(1)}, bf16[256,896]{1,0:T(8,128)(2,1)S(1)}, bf16[7424,896]{1,0:T(8,128)(2,1)}...) while((s32[]{:T(128)}, bf16[4,256,224]{1,2,0:T(8,128)(2,1)}, ...), condition=%wide.region_32.33_spmd, body=%wide.region_29.32_spmd.sunk | while | flops 1718148608 | bytes 32561836 | solution.py:243
  (445 shorter events, 609.5 us)
Async XLA Ops:
  7.2 729.9 %reduce-scatter.2.cloned.1.call-start = ((), (), s32[]{:S(2)}) async-start(), calls=%async_computation.1 | async-start | bytes 4587520 | tf_op jit(solution)/shard_map/reduce_scatter | solution.py:178
  8.6 62.8 %collective-permute-start.1 = (bf16[3,896]{1,0:T(4,128)(2,1)}, bf16[3,896]{1,0:T(4,128)(2,1)}, u32[]{:S(2)}, u32[]{:S(2)}) collective-permute-start(bf16[3,896]{1,0:T(4,128)(2,1)} %slice.131), channel_id=1, source_target_pairs={{0,4},{4,8},{8,12},{12,16},{16,20},{20,24},{24,28},{28,32},{32,36}... | collective-permute-start | bytes 16136 | tf_op jit(solution)/shard_map/ppermute | solution.py:16
  11.4 57.8 %collective-permute-start.2 = (bf16[3,128]{0,1:T(8,128)(2,1)S(1)}, bf16[3,128]{0,1:T(8,128)(2,1)}, u32[]{:S(2)}, u32[]{:S(2)}) collective-permute-start(bf16[3,128]{0,1:T(8,128)(2,1)S(1)} %copy.92), channel_id=1, source_target_pairs={{0,4},{4,8},{8,12},{12,16},{16,20},{20,24},{24,28},{28,32},{32,36}... | collective-permute-start | bytes 2312 | tf_op jit(solution)/shard_map/ppermute | solution.py:16
  496.6 447.3 %all-gather.2.cloned.1.call-start = ((), (), s32[]{:S(2)}) async-start(), calls=%async_computation.2 | async-start | bytes 2293760 | tf_op jit(solution)/shard_map/all_gather | solution.py:189
  498.6 28.5 %collective-permute-start.4 = (bf16[256,896]{1,0:T(8,128)(2,1)}, bf16[256,896]{1,0:T(8,128)(2,1)}, u32[]{:S(2)}, u32[]{:S(2)}) collective-permute-start(bf16[256,896]{1,0:T(8,128)(2,1)} %param.47), channel_id=1, source_target_pairs={{4,0},{8,4},{12,8},{16,12},{20,16},{24,20},{28,24},{32,28},{36,32}... | collective-permute-start | bytes 1376264 | tf_op jit(solution)/shard_map/ppermute | solution.py:16
  506.3 32.7 %collective-permute-start.6 = (bf16[256,896]{1,0:T(8,128)(2,1)}, bf16[256,896]{1,0:T(8,128)(2,1)}, u32[]{:S(2)}, u32[]{:S(2)}) collective-permute-start(bf16[256,896]{1,0:T(8,128)(2,1)} %param.47), channel_id=1, source_target_pairs={{8,0},{12,4},{16,8},{20,12},{24,16},{28,20},{32,24},{36,28},{40,32... | collective-permute-start | bytes 1376264 | tf_op jit(solution)/shard_map/ppermute | solution.py:16
  512.3 30.4 %collective-permute-start.7 = (bf16[256,896]{1,0:T(8,128)(2,1)}, bf16[256,896]{1,0:T(8,128)(2,1)}, u32[]{:S(2)}, u32[]{:S(2)}) collective-permute-start(bf16[256,896]{1,0:T(8,128)(2,1)} %param.47), channel_id=1, source_target_pairs={{0,12},{4,16},{8,20},{12,24},{16,28},{20,32},{24,36},{28,40},{32,4... | collective-permute-start | bytes 1376264 | tf_op jit(solution)/shard_map/ppermute | solution.py:16
  519.1 42.0 %collective-permute-start.8 = (bf16[256,896]{1,0:T(8,128)(2,1)}, bf16[256,896]{1,0:T(8,128)(2,1)S(1)}, u32[]{:S(2)}, u32[]{:S(2)}) collective-permute-start(bf16[256,896]{1,0:T(8,128)(2,1)} %param.47), channel_id=1, source_target_pairs={{12,0},{16,4},{20,8},{24,12},{28,16},{32,20},{36,24},{40,28},{44,3... | collective-permute-start | bytes 1376264 | tf_op jit(solution)/shard_map/ppermute | solution.py:16
  527.1 36.7 %collective-permute-start.9 = (bf16[256,896]{1,0:T(8,128)(2,1)}, bf16[256,896]{1,0:T(8,128)(2,1)S(1)}, u32[]{:S(2)}, u32[]{:S(2)}) collective-permute-start(bf16[256,896]{1,0:T(8,128)(2,1)} %param.47), channel_id=1, source_target_pairs={{0,16},{4,20},{8,24},{12,28},{16,32},{20,36},{24,40},{28,44},{32,4... | collective-permute-start | bytes 1376264 | tf_op jit(solution)/shard_map/ppermute | solution.py:16
  530.8 52.0 %collective-permute-start.10 = (bf16[256,896]{1,0:T(8,128)(2,1)}, bf16[256,896]{1,0:T(8,128)(2,1)S(1)}, u32[]{:S(2)}, u32[]{:S(2)}) collective-permute-start(bf16[256,896]{1,0:T(8,128)(2,1)} %param.47), channel_id=1, source_target_pairs={{16,0},{20,4},{24,8},{28,12},{32,16},{36,20},{40,24},{44,28},{48,3... | collective-permute-start | bytes 1376264 | tf_op jit(solution)/shard_map/ppermute | solution.py:16
  539.0 49.3 %collective-permute-start.11 = (bf16[256,896]{1,0:T(8,128)(2,1)}, bf16[256,896]{1,0:T(8,128)(2,1)S(1)}, u32[]{:S(2)}, u32[]{:S(2)}) collective-permute-start(bf16[256,896]{1,0:T(8,128)(2,1)} %param.47), channel_id=1, source_target_pairs={{0,20},{4,24},{8,28},{12,32},{16,36},{20,40},{24,44},{28,48},{32,5... | collective-permute-start | bytes 1376264 | tf_op jit(solution)/shard_map/ppermute | solution.py:16
  542.7 48.3 %collective-permute-start.12 = (bf16[256,896]{1,0:T(8,128)(2,1)}, bf16[256,896]{1,0:T(8,128)(2,1)S(1)}, u32[]{:S(2)}, u32[]{:S(2)}) collective-permute-start(bf16[256,896]{1,0:T(8,128)(2,1)} %param.47), channel_id=1, source_target_pairs={{20,0},{24,4},{28,8},{32,12},{36,16},{40,20},{44,24},{48,28},{52,3... | collective-permute-start | bytes 1376264 | tf_op jit(solution)/shard_map/ppermute | solution.py:16
  561.1 36.8 %collective-permute-start.13 = (bf16[256,896]{1,0:T(8,128)(2,1)}, bf16[256,896]{1,0:T(8,128)(2,1)S(1)}, u32[]{:S(2)}, u32[]{:S(2)}) collective-permute-start(bf16[256,896]{1,0:T(8,128)(2,1)} %param.47), channel_id=1, source_target_pairs={{0,24},{4,28},{8,32},{12,36},{16,40},{20,44},{24,48},{28,52},{32,5... | collective-permute-start | bytes 1376264 | tf_op jit(solution)/shard_map/ppermute | solution.py:16
  563.8 38.3 %collective-permute-start.14 = (bf16[256,896]{1,0:T(8,128)(2,1)}, bf16[256,896]{1,0:T(8,128)(2,1)S(1)}, u32[]{:S(2)}, u32[]{:S(2)}) collective-permute-start(bf16[256,896]{1,0:T(8,128)(2,1)} %param.47), channel_id=1, source_target_pairs={{24,0},{28,4},{32,8},{36,12},{40,16},{44,20},{48,24},{52,28},{56,3... | collective-permute-start | bytes 1376264 | tf_op jit(solution)/shard_map/ppermute | solution.py:16
  631.8 131.4 %collective-permute-start.21 = (bf16[256,896]{1,0:T(8,128)(2,1)}, bf16[256,896]{1,0:T(8,128)(2,1)}, u32[]{:S(2)}, u32[]{:S(2)}) collective-permute-start(bf16[256,896]{1,0:T(8,128)(2,1)} %param.49), channel_id=1, source_target_pairs={{0,4},{4,8},{8,12},{12,16},{16,20},{20,24},{24,28},{28,32},{32,36}... | collective-permute-start | bytes 1376264 | tf_op jit(solution)/shard_map/ppermute | solution.py:16
  639.1 35.7 %collective-permute-start.35 = (bf16[256,896]{1,0:T(8,128)(2,1)S(1)}, bf16[256,896]{1,0:T(8,128)(2,1)S(1)}, u32[]{:S(2)}, u32[]{:S(2)}) collective-permute-start(bf16[256,896]{1,0:T(8,128)(2,1)S(1)} %copy-done.4), channel_id=1, source_target_pairs={{12,0},{16,4},{20,8},{24,12},{28,16},{32,20},{36,24},{40,28},{44,3... | collective-permute-start | bytes 1376264 | tf_op jit(solution)/shard_map/ppermute | solution.py:16
  646.0 31.6 %collective-permute-start.36 = (bf16[256,896]{1,0:T(8,128)(2,1)S(1)}, bf16[256,896]{1,0:T(8,128)(2,1)S(1)}, u32[]{:S(2)}, u32[]{:S(2)}) collective-permute-start(bf16[256,896]{1,0:T(8,128)(2,1)S(1)} %copy-done.4), channel_id=1, source_target_pairs={{0,16},{4,20},{8,24},{12,28},{16,32},{20,36},{24,40},{28,44},{32,4... | collective-permute-start | bytes 1376264 | tf_op jit(solution)/shard_map/ppermute | solution.py:16
  649.0 40.3 %collective-permute-start.37 = (bf16[256,896]{1,0:T(8,128)(2,1)S(1)}, bf16[256,896]{1,0:T(8,128)(2,1)S(1)}, u32[]{:S(2)}, u32[]{:S(2)}) collective-permute-start(bf16[256,896]{1,0:T(8,128)(2,1)S(1)} %copy-done.4), channel_id=1, source_target_pairs={{16,0},{20,4},{24,8},{28,12},{32,16},{36,20},{40,24},{44,28},{48,3... | collective-permute-start | bytes 1376264 | tf_op jit(solution)/shard_map/ppermute | solution.py:16
  655.9 50.2 %collective-permute-start.38 = (bf16[256,896]{1,0:T(8,128)(2,1)S(1)}, bf16[256,896]{1,0:T(8,128)(2,1)S(1)}, u32[]{:S(2)}, u32[]{:S(2)}) collective-permute-start(bf16[256,896]{1,0:T(8,128)(2,1)S(1)} %copy-done.4), channel_id=1, source_target_pairs={{0,20},{4,24},{8,28},{12,32},{16,36},{20,40},{24,44},{28,48},{32,5... | collective-permute-start | bytes 1376264 | tf_op jit(solution)/shard_map/ppermute | solution.py:16
  674.8 35.0 %collective-permute-start.39 = (bf16[256,896]{1,0:T(8,128)(2,1)S(1)}, bf16[256,896]{1,0:T(8,128)(2,1)S(1)}, u32[]{:S(2)}, u32[]{:S(2)}) collective-permute-start(bf16[256,896]{1,0:T(8,128)(2,1)S(1)} %copy-done.4), channel_id=1, source_target_pairs={{20,0},{24,4},{28,8},{32,12},{36,16},{40,20},{44,24},{48,28},{52,3... | collective-permute-start | bytes 1376264 | tf_op jit(solution)/shard_map/ppermute | solution.py:16
  677.6 35.8 %collective-permute-start.40 = (bf16[256,896]{1,0:T(8,128)(2,1)S(1)}, bf16[256,896]{1,0:T(8,128)(2,1)S(1)}, u32[]{:S(2)}, u32[]{:S(2)}) collective-permute-start(bf16[256,896]{1,0:T(8,128)(2,1)S(1)} %copy-done.4), channel_id=1, source_target_pairs={{0,24},{4,28},{8,32},{12,36},{16,40},{20,44},{24,48},{28,52},{32,5... | collective-permute-start | bytes 1376264 | tf_op jit(solution)/shard_map/ppermute | solution.py:16
  689.3 33.4 %collective-permute-start.41 = (bf16[256,896]{1,0:T(8,128)(2,1)S(1)}, bf16[256,896]{1,0:T(8,128)(2,1)S(1)}, u32[]{:S(2)}, u32[]{:S(2)}) collective-permute-start(bf16[256,896]{1,0:T(8,128)(2,1)S(1)} %copy-done.4), channel_id=1, source_target_pairs={{24,0},{28,4},{32,8},{36,12},{40,16},{44,20},{48,24},{52,28},{56,3... | collective-permute-start | bytes 1376264 | tf_op jit(solution)/shard_map/ppermute | solution.py:16
  767.0 33.1 %collective-permute-start.27 = (bf16[256,896]{1,0:T(8,128)(2,1)}, bf16[256,896]{1,0:T(8,128)(2,1)S(1)}, u32[]{:S(2)}, u32[]{:S(2)}) collective-permute-start(bf16[256,896]{1,0:T(8,128)(2,1)} %param.49), channel_id=1, source_target_pairs={{0,28},{4,32},{8,36},{12,40},{16,44},{20,48},{24,52},{28,56},{32,6... | collective-permute-start | bytes 1376264 | tf_op jit(solution)/shard_map/ppermute | solution.py:16
  769.7 39.5 %collective-permute-start.28 = (bf16[256,896]{1,0:T(8,128)(2,1)}, bf16[256,896]{1,0:T(8,128)(2,1)S(1)}, u32[]{:S(2)}, u32[]{:S(2)}) collective-permute-start(bf16[256,896]{1,0:T(8,128)(2,1)} %param.49), channel_id=1, source_target_pairs={{0,32},{4,36},{8,40},{12,44},{16,48},{20,52},{24,56},{28,60},{32,6... | collective-permute-start | bytes 1376264 | tf_op jit(solution)/shard_map/ppermute | solution.py:16
  774.0 55.3 %collective-permute-start.29 = (bf16[256,896]{1,0:T(8,128)(2,1)}, bf16[256,896]{1,0:T(8,128)(2,1)S(1)}, u32[]{:S(2)}, u32[]{:S(2)}) collective-permute-start(bf16[256,896]{1,0:T(8,128)(2,1)} %param.49), channel_id=1, source_target_pairs={{0,36},{4,40},{8,44},{12,48},{16,52},{20,56},{24,60},{28,64},{32,6... | collective-permute-start | bytes 1376264 | tf_op jit(solution)/shard_map/ppermute | solution.py:16
  781.5 50.9 %collective-permute-start.48 = (bf16[256,896]{1,0:T(8,128)(2,1)}, bf16[256,896]{1,0:T(8,128)(2,1)S(1)}, u32[]{:S(2)}, u32[]{:S(2)}) collective-permute-start(bf16[256,896]{1,0:T(8,128)(2,1)} %param.50), channel_id=1, source_target_pairs={{0,4},{4,8},{8,12},{12,16},{16,20},{20,24},{24,28},{28,32},{32,36}... | collective-permute-start | bytes 1376264 | tf_op jit(solution)/shard_map/ppermute | solution.py:16
  788.0 65.1 %collective-permute-start.49 = (bf16[256,896]{1,0:T(8,128)(2,1)}, bf16[256,896]{1,0:T(8,128)(2,1)S(1)}, u32[]{:S(2)}, u32[]{:S(2)}) collective-permute-start(bf16[256,896]{1,0:T(8,128)(2,1)} %param.50), channel_id=1, source_target_pairs={{0,8},{4,12},{8,16},{12,20},{16,24},{20,28},{24,32},{28,36},{32,40... | collective-permute-start | bytes 1376264 | tf_op jit(solution)/shard_map/ppermute | solution.py:16
  800.0 55.8 %collective-permute-start.50 = (bf16[256,896]{1,0:T(8,128)(2,1)}, bf16[256,896]{1,0:T(8,128)(2,1)S(1)}, u32[]{:S(2)}, u32[]{:S(2)}) collective-permute-start(bf16[256,896]{1,0:T(8,128)(2,1)} %param.50), channel_id=1, source_target_pairs={{0,12},{4,16},{8,20},{12,24},{16,28},{20,32},{24,36},{28,40},{32,4... | collective-permute-start | bytes 1376264 | tf_op jit(solution)/shard_map/ppermute | solution.py:16
  809.2 49.4 %collective-permute-start.51 = (bf16[256,896]{1,0:T(8,128)(2,1)}, bf16[256,896]{1,0:T(8,128)(2,1)S(1)}, u32[]{:S(2)}, u32[]{:S(2)}) collective-permute-start(bf16[256,896]{1,0:T(8,128)(2,1)} %param.50), channel_id=1, source_target_pairs={{0,16},{4,20},{8,24},{12,28},{16,32},{20,36},{24,40},{28,44},{32,4... | collective-permute-start | bytes 1376264 | tf_op jit(solution)/shard_map/ppermute | solution.py:16
  829.3 35.8 %collective-permute-start.52 = (bf16[256,896]{1,0:T(8,128)(2,1)}, bf16[256,896]{1,0:T(8,128)(2,1)S(1)}, u32[]{:S(2)}, u32[]{:S(2)}) collective-permute-start(bf16[256,896]{1,0:T(8,128)(2,1)} %param.50), channel_id=1, source_target_pairs={{0,20},{4,24},{8,28},{12,32},{16,36},{20,40},{24,44},{28,48},{32,5... | collective-permute-start | bytes 1376264 | tf_op jit(solution)/shard_map/ppermute | solution.py:16
  832.4 33.5 %collective-permute-start.53 = (bf16[256,896]{1,0:T(8,128)(2,1)}, bf16[256,896]{1,0:T(8,128)(2,1)S(1)}, u32[]{:S(2)}, u32[]{:S(2)}) collective-permute-start(bf16[256,896]{1,0:T(8,128)(2,1)} %param.50), channel_id=1, source_target_pairs={{0,24},{4,28},{8,32},{12,36},{16,40},{20,44},{24,48},{28,52},{32,5... | collective-permute-start | bytes 1376264 | tf_op jit(solution)/shard_map/ppermute | solution.py:16
  858.6 84.4 %collective-permute-start.56 = (bf16[256,896]{1,0:T(8,128)(2,1)S(1)}, bf16[256,896]{1,0:T(8,128)(2,1)S(1)}, u32[]{:S(2)}, u32[]{:S(2)}) collective-permute-start(bf16[256,896]{1,0:T(8,128)(2,1)S(1)} %copy-done.5), channel_id=1, source_target_pairs={{0,36},{4,40},{8,44},{12,48},{16,52},{20,56},{24,60},{28,64},{32,6... | collective-permute-start | bytes 1376264 | tf_op jit(solution)/shard_map/ppermute | solution.py:16
  (81 other events, 2917.9 us)
Sparse Core Ops, SparseCore 0:
  496.7 39.0 reduce-scatter.1
  740.5 26.4 all-gather.1
where the time goes:
time: 1030 us; the launch traced here: 1020 us
  waiting for transfers between devices  440 us (43%)
  starting transfers between devices  315 us (31%)
  local copies, waits for them, and re-layouts  98.2 us (10%)
  matrix products  80.6 us (8%)
  other arithmetic  51.4 us (5%)
  between operations  19 us (2%)
  blocking collectives  10.6 us (1%)
    ppermute x87, waiting for transfers between devices, shifted_2(): lax.ppermute(value, axis, [(source, source + steps) for source in range(i...  440 us
    ppermute x87, starting transfers between devices, shifted_2(): lax.ppermute(value, axis, [(source, source + steps) for source in range(i...  315 us
    unnamed x109, local copies, waits for them, and re-layouts  65.1 us
    dot_general x4, matrix products, attend(): jnp.dot(probs, value_head, preferred_element_type=jnp.float32)  25.7 us
    unnamed x28, other arithmetic  21.4 us
    dot_general x4, matrix products, attend(): lax.dot_general(query_head, key_head, (((1,), (1,)), ((), ())), preferred...  20.6 us
  transfers between devices with their start and end apart: 89, of which 38 were waited for; matrix products, arithmetic and copies ran while one was open for 12% of the time, Pallas kernels for 0%

commit v1 on v0

--- a/solution.py
+++ b/solution.py
@@ -149,10 +149,14 @@
     )
     chain_decay = jnp.where(starts_here, jnp.zeros_like(whole_decay), whole_decay)
 
-    def relay(turn, incoming):
-        return shifted_2(chain_decay[:, None, None] * incoming + chain_state, "seq", 1)
-
-    carried = lax.fori_loop(0, seq_count - 1, relay, jnp.zeros_like(chain_state))
+    scan_decay, scan_state = chain_decay, chain_state
+    distance = 1
+    while distance <= reach and distance < seq_count:
+        prior_decay, prior_state = shifted_2((scan_decay, scan_state), "seq", distance)
+        scan_state = scan_decay[:, None, None] * prior_state + scan_state
+        scan_decay = scan_decay * prior_decay
+        distance *= 2
+    carried = shifted_2(scan_state, "seq", 1)
     continuing = position[0] > 0
     replace = (jnp.arange(prompts, dtype=jnp.int32) == segment[0]) & continuing
     initial = jnp.where(replace[:, None, None, None], carried[None], ssm_cache)

time: 1030 us -> 702 us (0.68)
  waiting for transfers between devices: 440 us -> 174 us
  starting transfers between devices: 315 us -> 275 us
  other arithmetic: 51.4 us -> 30.9 us
    ppermute x87 -> x64, waiting for transfers between devices: 440 us -> 174 us  [shifted_2(): lax.ppermute(value, axis, [(source, source + steps) for source in range(i...]
    ppermute x87 -> x64, starting transfers between devices: 315 us -> 275 us  [shifted_2(): lax.ppermute(value, axis, [(source, source + steps) for source in range(i...]
    unnamed x28, other arithmetic: 21.4 us -> 4.03 us
    unnamed x109 -> x81, local copies, waits for them, and re-layouts: 65.1 us -> 65.2 us
  transfers between devices with their start and end apart: 89 -> 66, of which waited for: 38 -> 14; matrix products, arithmetic and copies ran while one was open for 12% -> 16% of each run, Pallas kernels for 0% -> 0%
where the time goes in v1:
time: 702 us; the launch traced here: 692 us
  starting transfers between devices  275 us (39%)
  waiting for transfers between devices  174 us (25%)
  local copies, waits for them, and re-layouts  96.9 us (14%)
  matrix products  82.9 us (12%)
  other arithmetic  30.9 us (4%)
  between operations  19.1 us (3%)
  blocking collectives  10.6 us (2%)
    ppermute x64, starting transfers between devices, shifted_2(): lax.ppermute(value, axis, [(source, source + steps) for source in range(i...  275 us
    ppermute x64, waiting for transfers between devices, shifted_2(): lax.ppermute(value, axis, [(source, source + steps) for source in range(i...  174 us
    unnamed x81, local copies, waits for them, and re-layouts  65.2 us
    dot_general x4, matrix products, attend(): jnp.dot(probs, value_head, preferred_element_type=jnp.float32)  25.8 us
    dot_general x4, matrix products, attend(): lax.dot_general(query_head, key_head, (((1,), (1,)), ((), ())), preferred...  20.8 us
  transfers between devices with their start and end apart: 66, of which 14 were waited for; matrix products, arithmetic and copies ran while one was open for 16% of the time, Pallas kernels for 0%

profile of v1, /device:TPU:16, one launch (start us, length us, event | category | flops | bytes accessed | tf_op | source)
XLA Modules:
  0.0 691.7 jit_solution(182412171611824682)
XLA Ops:
  61.5 7.1 %collective-permute-done.5 = f32[14,64,64]{2,1,0:T(8,128)S(1)} collective-permute-done((f32[14,64,64]{2,1,0:T(8,128)S(1)}, f32[14,64,64]{2,1,0:T(8,128)S(1)}, u32[]{:S(2)}, u32[]{:S(2)}) %collective-permute-start.5) | collective-permute-done | bytes 229408 | tf_op jit(solution)/shard_map/ppermute | solution.py:16
  76.0 7.6 %collective-permute-done.3 = f32[14]{0:T(128)S(1)} collective-permute-done((f32[14]{0:T(128)S(1)}, f32[14]{0:T(128)S(1)}, u32[]{:S(2)}, u32[]{:S(2)}) %collective-permute-start.3) | collective-permute-done | bytes 88 | tf_op jit(solution)/shard_map/ppermute | solution.py:16
  96.1 10.2 %collective-permute-done.7 = f32[14,64,64]{2,1,0:T(8,128)S(1)} collective-permute-done((f32[14,64,64]{2,1,0:T(8,128)S(1)}, f32[14,64,64]{2,1,0:T(8,128)S(1)}, u32[]{:S(2)}, u32[]{:S(2)}) %collective-permute-start.7) | collective-permute-done | bytes 229408 | tf_op jit(solution)/shard_map/ppermute | solution.py:16
  122.0 6.8 collective-permute-done.9
  132.9 8.4 %copy.96 = f32[16,64,14,64]{1,0,3,2:T(8,128)} copy(f32[16,64,14,64]{1,3,2,0:T(8,128)S(1)} %select_bitcast_fusion) | data formatting | bytes 7340032 | tf_op jit(solution)/shard_map/transpose | solution.py:166
  141.3 7.3 %reshape.581 = f32[1024,896]{0,1:T(8,128)} reshape(f32[16,64,14,64]{1,0,3,2:T(8,128)} %copy.96) | data formatting | bytes 7340032 | tf_op jit(solution)/shard_map/reshape | solution.py:166
  152.7 10.6 %psum.7 = f32[256]{0:T(256)S(1)} all-reduce(f32[256]{0:T(256)S(1)} %get-tuple-element.144), channel_id=1, replica_groups=mesh['seq'=32,'tp'=4] {'tp'}, use_global_device_ids=true, to_apply=%region_6.7 | all-reduce | flops 256 | bytes 2048 | tf_op jit(solution)/shard_map/psum | solution.py:177
  163.6 6.8 fusion.99
  180.1 6.0 collective-permute-start.13
  204.8 6.3 collective-permute-start.17
  223.1 11.6 %collective-permute-done.15 = bf16[256,896]{1,0:T(8,128)(2,1)S(1)} collective-permute-done((bf16[256,896]{1,0:T(8,128)(2,1)}, bf16[256,896]{1,0:T(8,128)(2,1)S(1)}, u32[]{:S(2)}, u32[]{:S(2)}) %collective-permute-start.15) | collective-permute-done | bytes 458784 | tf_op jit(solution)/shard_map/ppermute | solution.py:16
  239.7 16.0 %collective-permute-start.21 = (bf16[256,896]{1,0:T(8,128)(2,1)}, bf16[256,896]{1,0:T(8,128)(2,1)S(1)}, u32[]{:S(2)}, u32[]{:S(2)}) collective-permute-start(bf16[256,896]{1,0:T(8,128)(2,1)} %param.45), channel_id=1, source_target_pairs={{24,0},{28,4},{32,8},{36,12},{40,16},{44,20},{48,24},{52,28},{56,3... | collective-permute-start | bytes 1376264 | tf_op jit(solution)/shard_map/ppermute | solution.py:16
  278.8 6.5 collective-permute-start.27
  312.3 6.0 collective-permute-start.42
  331.7 16.1 %collective-permute-done.42 = bf16[256,896]{1,0:T(8,128)(2,1)S(1)} collective-permute-done((bf16[256,896]{1,0:T(8,128)(2,1)S(1)}, bf16[256,896]{1,0:T(8,128)(2,1)S(1)}, u32[]{:S(2)}, u32[]{:S(2)}) %collective-permute-start.42) | collective-permute-done | bytes 458784 | tf_op jit(solution)/shard_map/ppermute | solution.py:16
  350.6 10.9 %collective-permute-start.47 = (bf16[256,896]{1,0:T(8,128)(2,1)S(1)}, bf16[256,896]{1,0:T(8,128)(2,1)S(1)}, u32[]{:S(2)}, u32[]{:S(2)}) collective-permute-start(bf16[256,896]{1,0:T(8,128)(2,1)S(1)} %copy-done.4), channel_id=1, source_target_pairs={{0,24},{4,28},{8,32},{12,36},{16,40},{20,44},{24,48},{28,52},{32,5... | collective-permute-start | bytes 1376264 | tf_op jit(solution)/shard_map/ppermute | solution.py:16
  362.3 16.1 %collective-permute-start.48 = (bf16[256,896]{1,0:T(8,128)(2,1)S(1)}, bf16[256,896]{1,0:T(8,128)(2,1)S(1)}, u32[]{:S(2)}, u32[]{:S(2)}) collective-permute-start(bf16[256,896]{1,0:T(8,128)(2,1)S(1)} %copy-done.4), channel_id=1, source_target_pairs={{24,0},{28,4},{32,8},{36,12},{40,16},{44,20},{48,24},{52,28},{56,3... | collective-permute-start | bytes 1376264 | tf_op jit(solution)/shard_map/ppermute | solution.py:16
  386.4 8.6 %collective-permute-start.51 = (bf16[256,896]{1,0:T(8,128)(2,1)S(1)}, bf16[256,896]{1,0:T(8,128)(2,1)}, u32[]{:S(2)}, u32[]{:S(2)}) collective-permute-start(bf16[256,896]{1,0:T(8,128)(2,1)S(1)} %copy-done.4), channel_id=1, source_target_pairs={{0,32},{4,36},{8,40},{12,44},{16,48},{20,52},{24,56},{28,60},{32,6... | collective-permute-start | bytes 1376264 | tf_op jit(solution)/shard_map/ppermute | solution.py:16
  447.1 6.6 collective-permute-start.36
  461.0 11.3 %collective-permute-start.56 = (bf16[256,896]{1,0:T(8,128)(2,1)}, bf16[256,896]{1,0:T(8,128)(2,1)S(1)}, u32[]{:S(2)}, u32[]{:S(2)}) collective-permute-start(bf16[256,896]{1,0:T(8,128)(2,1)} %param.48), channel_id=1, source_target_pairs={{0,8},{4,12},{8,16},{12,20},{16,24},{20,28},{24,32},{28,36},{32,40... | collective-permute-start | bytes 1376264 | tf_op jit(solution)/shard_map/ppermute | solution.py:16
  473.1 8.3 %collective-permute-start.57 = (bf16[256,896]{1,0:T(8,128)(2,1)}, bf16[256,896]{1,0:T(8,128)(2,1)S(1)}, u32[]{:S(2)}, u32[]{:S(2)}) collective-permute-start(bf16[256,896]{1,0:T(8,128)(2,1)} %param.48), channel_id=1, source_target_pairs={{0,12},{4,16},{8,20},{12,24},{16,28},{20,32},{24,36},{28,40},{32,4... | collective-permute-start | bytes 1376264 | tf_op jit(solution)/shard_map/ppermute | solution.py:16
  482.3 10.1 %collective-permute-start.58 = (bf16[256,896]{1,0:T(8,128)(2,1)}, bf16[256,896]{1,0:T(8,128)(2,1)S(1)}, u32[]{:S(2)}, u32[]{:S(2)}) collective-permute-start(bf16[256,896]{1,0:T(8,128)(2,1)} %param.48), channel_id=1, source_target_pairs={{0,16},{4,20},{8,24},{12,28},{16,32},{20,36},{24,40},{28,44},{32,4... | collective-permute-start | bytes 1376264 | tf_op jit(solution)/shard_map/ppermute | solution.py:16
  493.3 9.0 %collective-permute-done.36 = bf16[256,896]{1,0:T(8,128)(2,1)S(1)} collective-permute-done((bf16[256,896]{1,0:T(8,128)(2,1)}, bf16[256,896]{1,0:T(8,128)(2,1)S(1)}, u32[]{:S(2)}, u32[]{:S(2)}) %collective-permute-start.36) | collective-permute-done | bytes 458784 | tf_op jit(solution)/shard_map/ppermute | solution.py:16
  509.2 16.9 %collective-permute-done.56 = bf16[256,896]{1,0:T(8,128)(2,1)S(1)} collective-permute-done((bf16[256,896]{1,0:T(8,128)(2,1)}, bf16[256,896]{1,0:T(8,128)(2,1)S(1)}, u32[]{:S(2)}, u32[]{:S(2)}) %collective-permute-start.56) | collective-permute-done | bytes 458784 | tf_op jit(solution)/shard_map/ppermute | solution.py:16
  540.0 12.6 %collective-permute-done.61 = bf16[256,896]{1,0:T(8,128)(2,1)S(1)} collective-permute-done((bf16[256,896]{1,0:T(8,128)(2,1)S(1)}, bf16[256,896]{1,0:T(8,128)(2,1)S(1)}, u32[]{:S(2)}, u32[]{:S(2)}) %collective-permute-start.61) | collective-permute-done | bytes 458784 | tf_op jit(solution)/shard_map/ppermute | solution.py:16
  554.2 61.9 %collective-permute-done.63 = bf16[256,896]{1,0:T(8,128)(2,1)S(1)} collective-permute-done((bf16[256,896]{1,0:T(8,128)(2,1)S(1)}, bf16[256,896]{1,0:T(8,128)(2,1)S(1)}, u32[]{:S(2)}, u32[]{:S(2)}) %collective-permute-start.63) | collective-permute-done | bytes 458784 | tf_op jit(solution)/shard_map/ppermute | solution.py:16
  616.9 6.4 fusion.100
  625.9 56.4 %while.2 = (s32[]{:T(128)}, bf16[4,256,224]{1,2,0:T(8,128)(2,1)}, s32[4]{0:T(128)S(1)}, bf16[256,896]{1,0:T(8,128)(2,1)S(1)}, bf16[7424,896]{1,0:T(8,128)(2,1)},...) while((s32[]{:T(128)}, bf16[4,256,224]{1,2,0:T(8,128)(2,1)}, ...), condition=%wide.region_30.31_spmd, body=%wide.region_27.30_spmd.sunk | while | flops 1718148608 | bytes 32561836 | solution.py:247
  633.7 6.6 fusion.118
  648.0 6.6 fusion.118
  662.5 6.6 fusion.118
  676.2 6.1 fusion.118
  (345 shorter events, 332.1 us)
Async XLA Ops:
  7.2 403.0 %reduce-scatter.2.cloned.1.call-start = ((), (), s32[]{:S(2)}) async-start(), calls=%async_computation.1 | async-start | bytes 4587520 | tf_op jit(solution)/shard_map/reduce_scatter | solution.py:182
  8.0 41.1 %collective-permute-start = (bf16[3,896]{1,0:T(4,128)(2,1)S(1)}, bf16[3,896]{1,0:T(4,128)(2,1)S(1)}, u32[]{:S(2)}, u32[]{:S(2)}) collective-permute-start(bf16[3,896]{1,0:T(4,128)(2,1)S(1)} %slice.131), channel_id=1, source_target_pairs={{0,4},{4,8},{8,12},{12,16},{16,20},{20,24},{24,28},{28,32},{32,36}... | collective-permute-start | bytes 16136 | tf_op jit(solution)/shard_map/ppermute | solution.py:16
  10.8 37.3 %collective-permute-start.1 = (bf16[3,128]{0,1:T(8,128)(2,1)S(1)}, bf16[3,128]{0,1:T(8,128)(2,1)S(1)}, u32[]{:S(2)}, u32[]{:S(2)}) collective-permute-start(bf16[3,128]{0,1:T(8,128)(2,1)S(1)} %copy.92), channel_id=1, source_target_pairs={{0,4},{4,8},{8,12},{12,16},{16,20},{20,24},{24,28},{28,32},{32,36}... | collective-permute-start | bytes 2312 | tf_op jit(solution)/shard_map/ppermute | solution.py:16
  23.5 48.5 %collective-permute-start.2 = (f32[14]{0:T(128)S(1)}, f32[14]{0:T(128)S(1)}, u32[]{:S(2)}, u32[]{:S(2)}) collective-permute-start(f32[14]{0:T(128)S(1)} %get-tuple-element.112), channel_id=1, source_target_pairs={{0,4},{4,8},{8,12},{12,16},{16,20},{20,24},{24,28},{28,32},{32,36}... | collective-permute-start | bytes 176 | tf_op jit(solution)/shard_map/ppermute | solution.py:16
  170.4 446.5 %all-gather.2.cloned.1.call-start = ((), (), s32[]{:S(2)}) async-start(), calls=%async_computation.2 | async-start | bytes 2293760 | tf_op jit(solution)/shard_map/all_gather | solution.py:193
  180.1 32.8 %collective-permute-start.13 = (bf16[256,896]{1,0:T(8,128)(2,1)}, bf16[256,896]{1,0:T(8,128)(2,1)}, u32[]{:S(2)}, u32[]{:S(2)}) collective-permute-start(bf16[256,896]{1,0:T(8,128)(2,1)} %param.45), channel_id=1, source_target_pairs={{8,0},{12,4},{16,8},{20,12},{24,16},{28,20},{32,24},{36,28},{40,32... | collective-permute-start | bytes 1376264 | tf_op jit(solution)/shard_map/ppermute | solution.py:16
  186.1 30.5 %collective-permute-start.14 = (bf16[256,896]{1,0:T(8,128)(2,1)}, bf16[256,896]{1,0:T(8,128)(2,1)}, u32[]{:S(2)}, u32[]{:S(2)}) collective-permute-start(bf16[256,896]{1,0:T(8,128)(2,1)} %param.45), channel_id=1, source_target_pairs={{0,12},{4,16},{8,20},{12,24},{16,28},{20,32},{24,36},{28,40},{32,4... | collective-permute-start | bytes 1376264 | tf_op jit(solution)/shard_map/ppermute | solution.py:16
  193.2 41.5 %collective-permute-start.15 = (bf16[256,896]{1,0:T(8,128)(2,1)}, bf16[256,896]{1,0:T(8,128)(2,1)S(1)}, u32[]{:S(2)}, u32[]{:S(2)}) collective-permute-start(bf16[256,896]{1,0:T(8,128)(2,1)} %param.45), channel_id=1, source_target_pairs={{12,0},{16,4},{20,8},{24,12},{28,16},{32,20},{36,24},{40,28},{44,3... | collective-permute-start | bytes 1376264 | tf_op jit(solution)/shard_map/ppermute | solution.py:16
  201.0 38.7 %collective-permute-start.16 = (bf16[256,896]{1,0:T(8,128)(2,1)}, bf16[256,896]{1,0:T(8,128)(2,1)S(1)}, u32[]{:S(2)}, u32[]{:S(2)}) collective-permute-start(bf16[256,896]{1,0:T(8,128)(2,1)} %param.45), channel_id=1, source_target_pairs={{0,16},{4,20},{8,24},{12,28},{16,32},{20,36},{24,40},{28,44},{32,4... | collective-permute-start | bytes 1376264 | tf_op jit(solution)/shard_map/ppermute | solution.py:16
  204.8 51.7 %collective-permute-start.17 = (bf16[256,896]{1,0:T(8,128)(2,1)}, bf16[256,896]{1,0:T(8,128)(2,1)S(1)}, u32[]{:S(2)}, u32[]{:S(2)}) collective-permute-start(bf16[256,896]{1,0:T(8,128)(2,1)} %param.45), channel_id=1, source_target_pairs={{16,0},{20,4},{24,8},{28,12},{32,16},{36,20},{40,24},{44,28},{48,3... | collective-permute-start | bytes 1376264 | tf_op jit(solution)/shard_map/ppermute | solution.py:16
  212.9 49.1 %collective-permute-start.18 = (bf16[256,896]{1,0:T(8,128)(2,1)}, bf16[256,896]{1,0:T(8,128)(2,1)S(1)}, u32[]{:S(2)}, u32[]{:S(2)}) collective-permute-start(bf16[256,896]{1,0:T(8,128)(2,1)} %param.45), channel_id=1, source_target_pairs={{0,20},{4,24},{8,28},{12,32},{16,36},{20,40},{24,44},{28,48},{32,5... | collective-permute-start | bytes 1376264 | tf_op jit(solution)/shard_map/ppermute | solution.py:16
  216.7 48.1 %collective-permute-start.19 = (bf16[256,896]{1,0:T(8,128)(2,1)}, bf16[256,896]{1,0:T(8,128)(2,1)S(1)}, u32[]{:S(2)}, u32[]{:S(2)}) collective-permute-start(bf16[256,896]{1,0:T(8,128)(2,1)} %param.45), channel_id=1, source_target_pairs={{20,0},{24,4},{28,8},{32,12},{36,16},{40,20},{44,24},{48,28},{52,3... | collective-permute-start | bytes 1376264 | tf_op jit(solution)/shard_map/ppermute | solution.py:16
  234.6 36.3 %collective-permute-start.20 = (bf16[256,896]{1,0:T(8,128)(2,1)}, bf16[256,896]{1,0:T(8,128)(2,1)S(1)}, u32[]{:S(2)}, u32[]{:S(2)}) collective-permute-start(bf16[256,896]{1,0:T(8,128)(2,1)} %param.45), channel_id=1, source_target_pairs={{0,24},{4,28},{8,32},{12,36},{16,40},{20,44},{24,48},{28,52},{32,5... | collective-permute-start | bytes 1376264 | tf_op jit(solution)/shard_map/ppermute | solution.py:16
  239.7 35.5 %collective-permute-start.21 = (bf16[256,896]{1,0:T(8,128)(2,1)}, bf16[256,896]{1,0:T(8,128)(2,1)S(1)}, u32[]{:S(2)}, u32[]{:S(2)}) collective-permute-start(bf16[256,896]{1,0:T(8,128)(2,1)} %param.45), channel_id=1, source_target_pairs={{24,0},{28,4},{32,8},{36,12},{40,16},{44,20},{48,24},{52,28},{56,3... | collective-permute-start | bytes 1376264 | tf_op jit(solution)/shard_map/ppermute | solution.py:16
  305.0 131.0 %collective-permute-start.28 = (bf16[256,896]{1,0:T(8,128)(2,1)}, bf16[256,896]{1,0:T(8,128)(2,1)}, u32[]{:S(2)}, u32[]{:S(2)}) collective-permute-start(bf16[256,896]{1,0:T(8,128)(2,1)} %param.47), channel_id=1, source_target_pairs={{0,4},{4,8},{8,12},{12,16},{16,20},{20,24},{24,28},{28,32},{32,36}... | collective-permute-start | bytes 1376264 | tf_op jit(solution)/shard_map/ppermute | solution.py:16
  312.3 35.6 %collective-permute-start.42 = (bf16[256,896]{1,0:T(8,128)(2,1)S(1)}, bf16[256,896]{1,0:T(8,128)(2,1)S(1)}, u32[]{:S(2)}, u32[]{:S(2)}) collective-permute-start(bf16[256,896]{1,0:T(8,128)(2,1)S(1)} %copy-done.4), channel_id=1, source_target_pairs={{12,0},{16,4},{20,8},{24,12},{28,16},{32,20},{36,24},{40,28},{44,3... | collective-permute-start | bytes 1376264 | tf_op jit(solution)/shard_map/ppermute | solution.py:16
  319.1 31.5 %collective-permute-start.43 = (bf16[256,896]{1,0:T(8,128)(2,1)S(1)}, bf16[256,896]{1,0:T(8,128)(2,1)S(1)}, u32[]{:S(2)}, u32[]{:S(2)}) collective-permute-start(bf16[256,896]{1,0:T(8,128)(2,1)S(1)} %copy-done.4), channel_id=1, source_target_pairs={{0,16},{4,20},{8,24},{12,28},{16,32},{20,36},{24,40},{28,44},{32,4... | collective-permute-start | bytes 1376264 | tf_op jit(solution)/shard_map/ppermute | solution.py:16
  322.1 40.1 %collective-permute-start.44 = (bf16[256,896]{1,0:T(8,128)(2,1)S(1)}, bf16[256,896]{1,0:T(8,128)(2,1)S(1)}, u32[]{:S(2)}, u32[]{:S(2)}) collective-permute-start(bf16[256,896]{1,0:T(8,128)(2,1)S(1)} %copy-done.4), channel_id=1, source_target_pairs={{16,0},{20,4},{24,8},{28,12},{32,16},{36,20},{40,24},{44,28},{48,3... | collective-permute-start | bytes 1376264 | tf_op jit(solution)/shard_map/ppermute | solution.py:16
  329.0 50.2 %collective-permute-start.45 = (bf16[256,896]{1,0:T(8,128)(2,1)S(1)}, bf16[256,896]{1,0:T(8,128)(2,1)S(1)}, u32[]{:S(2)}, u32[]{:S(2)}) collective-permute-start(bf16[256,896]{1,0:T(8,128)(2,1)S(1)} %copy-done.4), channel_id=1, source_target_pairs={{0,20},{4,24},{8,28},{12,32},{16,36},{20,40},{24,44},{28,48},{32,5... | collective-permute-start | bytes 1376264 | tf_op jit(solution)/shard_map/ppermute | solution.py:16
  347.8 34.9 %collective-permute-start.46 = (bf16[256,896]{1,0:T(8,128)(2,1)S(1)}, bf16[256,896]{1,0:T(8,128)(2,1)S(1)}, u32[]{:S(2)}, u32[]{:S(2)}) collective-permute-start(bf16[256,896]{1,0:T(8,128)(2,1)S(1)} %copy-done.4), channel_id=1, source_target_pairs={{20,0},{24,4},{28,8},{32,12},{36,16},{40,20},{44,24},{48,28},{52,3... | collective-permute-start | bytes 1376264 | tf_op jit(solution)/shard_map/ppermute | solution.py:16
  350.6 35.8 %collective-permute-start.47 = (bf16[256,896]{1,0:T(8,128)(2,1)S(1)}, bf16[256,896]{1,0:T(8,128)(2,1)S(1)}, u32[]{:S(2)}, u32[]{:S(2)}) collective-permute-start(bf16[256,896]{1,0:T(8,128)(2,1)S(1)} %copy-done.4), channel_id=1, source_target_pairs={{0,24},{4,28},{8,32},{12,36},{16,40},{20,44},{24,48},{28,52},{32,5... | collective-permute-start | bytes 1376264 | tf_op jit(solution)/shard_map/ppermute | solution.py:16
  362.3 33.5 %collective-permute-start.48 = (bf16[256,896]{1,0:T(8,128)(2,1)S(1)}, bf16[256,896]{1,0:T(8,128)(2,1)S(1)}, u32[]{:S(2)}, u32[]{:S(2)}) collective-permute-start(bf16[256,896]{1,0:T(8,128)(2,1)S(1)} %copy-done.4), channel_id=1, source_target_pairs={{24,0},{28,4},{32,8},{36,12},{40,16},{44,20},{48,24},{52,28},{56,3... | collective-permute-start | bytes 1376264 | tf_op jit(solution)/shard_map/ppermute | solution.py:16
  439.7 33.4 %collective-permute-start.34 = (bf16[256,896]{1,0:T(8,128)(2,1)}, bf16[256,896]{1,0:T(8,128)(2,1)S(1)}, u32[]{:S(2)}, u32[]{:S(2)}) collective-permute-start(bf16[256,896]{1,0:T(8,128)(2,1)} %param.47), channel_id=1, source_target_pairs={{0,28},{4,32},{8,36},{12,40},{16,44},{20,48},{24,52},{28,56},{32,6... | collective-permute-start | bytes 1376264 | tf_op jit(solution)/shard_map/ppermute | solution.py:16
  442.5 39.8 %collective-permute-start.35 = (bf16[256,896]{1,0:T(8,128)(2,1)}, bf16[256,896]{1,0:T(8,128)(2,1)S(1)}, u32[]{:S(2)}, u32[]{:S(2)}) collective-permute-start(bf16[256,896]{1,0:T(8,128)(2,1)} %param.47), channel_id=1, source_target_pairs={{0,32},{4,36},{8,40},{12,44},{16,48},{20,52},{24,56},{28,60},{32,6... | collective-permute-start | bytes 1376264 | tf_op jit(solution)/shard_map/ppermute | solution.py:16
  447.1 55.3 %collective-permute-start.36 = (bf16[256,896]{1,0:T(8,128)(2,1)}, bf16[256,896]{1,0:T(8,128)(2,1)S(1)}, u32[]{:S(2)}, u32[]{:S(2)}) collective-permute-start(bf16[256,896]{1,0:T(8,128)(2,1)} %param.47), channel_id=1, source_target_pairs={{0,36},{4,40},{8,44},{12,48},{16,52},{20,56},{24,60},{28,64},{32,6... | collective-permute-start | bytes 1376264 | tf_op jit(solution)/shard_map/ppermute | solution.py:16
  454.5 50.9 %collective-permute-start.55 = (bf16[256,896]{1,0:T(8,128)(2,1)}, bf16[256,896]{1,0:T(8,128)(2,1)S(1)}, u32[]{:S(2)}, u32[]{:S(2)}) collective-permute-start(bf16[256,896]{1,0:T(8,128)(2,1)} %param.48), channel_id=1, source_target_pairs={{0,4},{4,8},{8,12},{12,16},{16,20},{20,24},{24,28},{28,32},{32,36}... | collective-permute-start | bytes 1376264 | tf_op jit(solution)/shard_map/ppermute | solution.py:16
  461.0 65.2 %collective-permute-start.56 = (bf16[256,896]{1,0:T(8,128)(2,1)}, bf16[256,896]{1,0:T(8,128)(2,1)S(1)}, u32[]{:S(2)}, u32[]{:S(2)}) collective-permute-start(bf16[256,896]{1,0:T(8,128)(2,1)} %param.48), channel_id=1, source_target_pairs={{0,8},{4,12},{8,16},{12,20},{16,24},{20,28},{24,32},{28,36},{32,40... | collective-permute-start | bytes 1376264 | tf_op jit(solution)/shard_map/ppermute | solution.py:16
  473.1 55.8 %collective-permute-start.57 = (bf16[256,896]{1,0:T(8,128)(2,1)}, bf16[256,896]{1,0:T(8,128)(2,1)S(1)}, u32[]{:S(2)}, u32[]{:S(2)}) collective-permute-start(bf16[256,896]{1,0:T(8,128)(2,1)} %param.48), channel_id=1, source_target_pairs={{0,12},{4,16},{8,20},{12,24},{16,28},{20,32},{24,36},{28,40},{32,4... | collective-permute-start | bytes 1376264 | tf_op jit(solution)/shard_map/ppermute | solution.py:16
  482.3 49.3 %collective-permute-start.58 = (bf16[256,896]{1,0:T(8,128)(2,1)}, bf16[256,896]{1,0:T(8,128)(2,1)S(1)}, u32[]{:S(2)}, u32[]{:S(2)}) collective-permute-start(bf16[256,896]{1,0:T(8,128)(2,1)} %param.48), channel_id=1, source_target_pairs={{0,16},{4,20},{8,24},{12,28},{16,32},{20,36},{24,40},{28,44},{32,4... | collective-permute-start | bytes 1376264 | tf_op jit(solution)/shard_map/ppermute | solution.py:16
  502.4 36.0 %collective-permute-start.59 = (bf16[256,896]{1,0:T(8,128)(2,1)}, bf16[256,896]{1,0:T(8,128)(2,1)S(1)}, u32[]{:S(2)}, u32[]{:S(2)}) collective-permute-start(bf16[256,896]{1,0:T(8,128)(2,1)} %param.48), channel_id=1, source_target_pairs={{0,20},{4,24},{8,28},{12,32},{16,36},{20,40},{24,44},{28,48},{32,5... | collective-permute-start | bytes 1376264 | tf_op jit(solution)/shard_map/ppermute | solution.py:16
  505.4 33.7 %collective-permute-start.60 = (bf16[256,896]{1,0:T(8,128)(2,1)}, bf16[256,896]{1,0:T(8,128)(2,1)S(1)}, u32[]{:S(2)}, u32[]{:S(2)}) collective-permute-start(bf16[256,896]{1,0:T(8,128)(2,1)} %param.48), channel_id=1, source_target_pairs={{0,24},{4,28},{8,32},{12,36},{16,40},{20,44},{24,48},{28,52},{32,5... | collective-permute-start | bytes 1376264 | tf_op jit(solution)/shard_map/ppermute | solution.py:16
  531.6 84.5 %collective-permute-start.63 = (bf16[256,896]{1,0:T(8,128)(2,1)S(1)}, bf16[256,896]{1,0:T(8,128)(2,1)S(1)}, u32[]{:S(2)}, u32[]{:S(2)}) collective-permute-start(bf16[256,896]{1,0:T(8,128)(2,1)S(1)} %copy-done.5), channel_id=1, source_target_pairs={{0,36},{4,40},{8,44},{12,48},{16,52},{20,56},{24,60},{28,64},{32,6... | collective-permute-start | bytes 1376264 | tf_op jit(solution)/shard_map/ppermute | solution.py:16
  (44 other events, 1881.2 us)
Sparse Core Ops, SparseCore 0:
  170.5 39.8 reduce-scatter.1
  413.5 26.5 all-gather.1

commit v2 on v1

--- a/solution.py
+++ b/solution.py
@@ -82,6 +82,14 @@
     seq_count = lax.axis_size("seq")
     reach = seq_count // 4 + 1
     first = seq_index * length
+    behind = jnp.stack([cache_keys, cache_values, new_keys, new_values])
+    forward = jnp.stack([cache_keys, cache_values])
+    behind_pieces, forward_pieces = [], []
+    for _ in range(reach):
+        behind = shifted_2(behind, "seq", 1)
+        forward = shifted_2(forward, "seq", -1)
+        behind_pieces.append(behind)
+        forward_pieces.append(forward)
     local_index = first + jnp.arange(length, dtype=jnp.int32)
     segment, begin, valid, onehot = locate(lengths, local_index)
     position = local_index - begin
@@ -209,10 +217,10 @@
     cache_pieces = [(cache_keys, cache_values, 0)]
     new_pieces = [(new_keys, new_values, 0)]
     for distance in range(1, reach + 1):
-        behind = shifted_2((cache_keys, cache_values, new_keys, new_values), "seq", distance)
+        behind = behind_pieces[distance - 1]
         cache_pieces.append((behind[0], behind[1], -distance))
         new_pieces.append((behind[2], behind[3], -distance))
-        forward = shifted_2((cache_keys, cache_values), "seq", -distance)
+        forward = forward_pieces[distance - 1]
         cache_pieces.append((forward[0], forward[1], distance))
     all_keys = jnp.concatenate(
         [entry[0] for entry in cache_pieces] + [entry[0] for entry in new_pieces], axis=0

time: 702 us -> 478 us (0.68)
  the two profiles are of different devices: /device:TPU:16 before, /device:TPU:24 now
where the time goes in v2:
time: 478 us; the launch traced here: 469 us
  waiting for transfers between devices  125 us (26%)
  starting transfers between devices  103 us (22%)
  local copies, waits for them, and re-layouts  93 us (19%)
  matrix products  81.5 us (17%)
  other arithmetic  34.8 us (7%)
  between operations  18.5 us (4%)
  blocking collectives  10.5 us (2%)
    ppermute x28, waiting for transfers between devices, shifted_2(): lax.ppermute(value, axis, [(source, source + steps) for source in range(i...  125 us
    ppermute x28, starting transfers between devices, shifted_2(): lax.ppermute(value, axis, [(source, source + steps) for source in range(i...  103 us
    unnamed x90, local copies, waits for them, and re-layouts  62 us
    dot_general x4, matrix products, attend(): jnp.dot(probs, value_head, preferred_element_type=jnp.float32)  25.8 us
    dot_general x4, matrix products, attend(): lax.dot_general(query_head, key_head, (((1,), (1,)), ((), ())), preferred...  20.6 us
    dot_general x6, matrix products, convolve(): jnp.dot(picks, cache[:, slot, :], preferred_element_type=jnp.float32)  10.7 us
    psum x1, blocking collectives, per_device(): squares = lax.psum(jnp.sum(gated * gated, axis=1), 'tp')  10.5 us
  transfers between devices with their start and end apart: 30, of which 17 were waited for; matrix products, arithmetic and copies ran while one was open for 27% of the time, Pallas kernels for 0%

profile of v2, /device:TPU:24, one launch (start us, length us, event | category | flops | bytes accessed | tf_op | source)
XLA Modules:
  0.0 468.5 jit_solution(15425498502018709823)
XLA Ops:
  63.2 9.1 %collective-permute-done.5 = f32[14,64,64]{2,1,0:T(8,128)S(1)} collective-permute-done((f32[14,64,64]{2,1,0:T(8,128)S(1)}, f32[14,64,64]{2,1,0:T(8,128)S(1)}, u32[]{:S(2)}, u32[]{:S(2)}) %collective-permute-start.5) | collective-permute-done | bytes 229408 | tf_op jit(solution)/shard_map/ppermute | solution.py:16
  79.0 8.1 %collective-permute-done.3 = f32[14]{0:T(128)S(1)} collective-permute-done((f32[14]{0:T(128)S(1)}, f32[14]{0:T(128)S(1)}, u32[]{:S(2)}, u32[]{:S(2)}) %collective-permute-start.3) | collective-permute-done | bytes 88 | tf_op jit(solution)/shard_map/ppermute | solution.py:16
  98.9 12.5 %collective-permute-done.7 = f32[14,64,64]{2,1,0:T(8,128)S(1)} collective-permute-done((f32[14,64,64]{2,1,0:T(8,128)S(1)}, f32[14,64,64]{2,1,0:T(8,128)S(1)}, u32[]{:S(2)}, u32[]{:S(2)}) %collective-permute-start.7) | collective-permute-done | bytes 229408 | tf_op jit(solution)/shard_map/ppermute | solution.py:16
  113.0 8.9 %collective-permute-done.8 = f32[14,64,64]{2,1,0:T(8,128)S(1)} collective-permute-done((f32[14,64,64]{2,1,0:T(8,128)S(1)}, f32[14,64,64]{2,1,0:T(8,128)S(1)}, u32[]{:S(2)}, u32[]{:S(2)}) %collective-permute-start.8) | collective-permute-done | bytes 229408 | tf_op jit(solution)/shard_map/ppermute | solution.py:16
  138.0 8.4 %copy.96 = f32[16,64,14,64]{1,0,3,2:T(8,128)} copy(f32[16,64,14,64]{1,3,2,0:T(8,128)S(1)} %select_bitcast_fusion) | data formatting | bytes 7340032 | tf_op jit(solution)/shard_map/transpose | solution.py:174
  146.4 7.4 %reshape.581 = f32[1024,896]{0,1:T(8,128)} reshape(f32[16,64,14,64]{1,0,3,2:T(8,128)} %copy.96) | data formatting | bytes 7340032 | tf_op jit(solution)/shard_map/reshape | solution.py:174
  157.6 10.5 %psum.7 = f32[256]{0:T(256)S(1)} all-reduce(f32[256]{0:T(256)S(1)} %get-tuple-element.198), channel_id=1, replica_groups=mesh['seq'=32,'tp'=4] {'tp'}, use_global_device_ids=true, to_apply=%region_6.7 | all-reduce | flops 256 | bytes 2048 | tf_op jit(solution)/shard_map/psum | solution.py:185
  168.3 6.9 %fusion.153 = f32[256,3584]{1,0:T(8,128)} fusion(bf16[256,896]{0,1:T(8,128)(2,1)S(1)} %fusion.41, bf16[896,3584]{1,0:T(8,128)(2,1)} %param.40), kind=kOutput, calls=%fused_computation.380 | convolution fusion | flops 1644167168 | bytes 10551296 | tf_op jit(solution)/shard_map/dot_general | solution.py:191
  177.4 5.8 %collective-permute-start.11 = (bf16[2,256,896]{2,1,0:T(8,128)(2,1)S(1)}, bf16[2,256,896]{2,1,0:T(8,128)(2,1)S(1)}, u32[]{:S(2)}, u32[]{:S(2)}) collective-permute-start(bf16[2,256,896]{2,1,0:T(8,128)(2,1)S(1)} %pad_maximum_fusion.1), channel_id=1, source_target_pairs={{4,0},{8,4},{12,8},{16,12},{20,16},{24,20},{28,24},{32,28},{36,32}... | collective-permute-start | bytes 2752520 | tf_op jit(solution)/shard_map/ppermute | solution.py:16
  183.1 19.1 %collective-permute-done.14 = bf16[4,256,896]{2,1,0:T(8,128)(2,1)S(1)} collective-permute-done((bf16[4,256,896]{2,1,0:T(8,128)(2,1)}, bf16[4,256,896]{2,1,0:T(8,128)(2,1)S(1)}, u32[]{:S(2)}, u32[]{:S(2)}) %collective-permute-start.14) | collective-permute-done | bytes 1835040 | tf_op jit(solution)/shard_map/ppermute | solution.py:16
  205.4 5.8 %collective-permute-start.13 = (bf16[2,256,896]{2,1,0:T(8,128)(2,1)S(1)}, bf16[2,256,896]{2,1,0:T(8,128)(2,1)S(1)}, u32[]{:S(2)}, u32[]{:S(2)}) collective-permute-start(bf16[2,256,896]{2,1,0:T(8,128)(2,1)S(1)} %collective-permute-done.11), channel_id=1, source_target_pairs={{4,0},{8,4},{12,8},{16,12},{20,16},{24,20},{28,24},{32,28},{36,32}... | collective-permute-start | bytes 2752520 | tf_op jit(solution)/shard_map/ppermute | solution.py:16
  211.1 10.9 %collective-permute-done.13 = bf16[2,256,896]{2,1,0:T(8,128)(2,1)S(1)} collective-permute-done((bf16[2,256,896]{2,1,0:T(8,128)(2,1)S(1)}, bf16[2,256,896]{2,1,0:T(8,128)(2,1)S(1)}, u32[]{:S(2)}, u32[]{:S(2)}) %collective-permute-start.13) | collective-permute-done | bytes 917536 | tf_op jit(solution)/shard_map/ppermute | solution.py:16
  222.0 5.9 %collective-permute-start.15 = (bf16[2,256,896]{2,1,0:T(8,128)(2,1)S(1)}, bf16[2,256,896]{2,1,0:T(8,128)(2,1)S(1)}, u32[]{:S(2)}, u32[]{:S(2)}) collective-permute-start(bf16[2,256,896]{2,1,0:T(8,128)(2,1)S(1)} %collective-permute-done.13), channel_id=1, source_target_pairs={{4,0},{8,4},{12,8},{16,12},{20,16},{24,20},{28,24},{32,28},{36,32}... | collective-permute-start | bytes 2752520 | tf_op jit(solution)/shard_map/ppermute | solution.py:16
  233.2 5.6 %collective-permute-done.15 = bf16[2,256,896]{2,1,0:T(8,128)(2,1)S(1)} collective-permute-done((bf16[2,256,896]{2,1,0:T(8,128)(2,1)S(1)}, bf16[2,256,896]{2,1,0:T(8,128)(2,1)S(1)}, u32[]{:S(2)}, u32[]{:S(2)}) %collective-permute-start.15) | collective-permute-done | bytes 917536 | tf_op jit(solution)/shard_map/ppermute | solution.py:16
  238.8 5.9 %collective-permute-start.17 = (bf16[2,256,896]{2,1,0:T(8,128)(2,1)S(1)}, bf16[2,256,896]{2,1,0:T(8,128)(2,1)S(1)}, u32[]{:S(2)}, u32[]{:S(2)}) collective-permute-start(bf16[2,256,896]{2,1,0:T(8,128)(2,1)S(1)} %collective-permute-done.15), channel_id=1, source_target_pairs={{4,0},{8,4},{12,8},{16,12},{20,16},{24,20},{28,24},{32,28},{36,32}... | collective-permute-start | bytes 2752520 | tf_op jit(solution)/shard_map/ppermute | solution.py:16
  244.7 10.9 %collective-permute-done.17 = bf16[2,256,896]{2,1,0:T(8,128)(2,1)S(1)} collective-permute-done((bf16[2,256,896]{2,1,0:T(8,128)(2,1)S(1)}, bf16[2,256,896]{2,1,0:T(8,128)(2,1)S(1)}, u32[]{:S(2)}, u32[]{:S(2)}) %collective-permute-start.17) | collective-permute-done | bytes 917536 | tf_op jit(solution)/shard_map/ppermute | solution.py:16
  255.6 16.2 %collective-permute-start.19 = (bf16[2,256,896]{2,1,0:T(8,128)(2,1)S(1)}, bf16[2,256,896]{2,1,0:T(8,128)(2,1)}, u32[]{:S(2)}, u32[]{:S(2)}) collective-permute-start(bf16[2,256,896]{2,1,0:T(8,128)(2,1)S(1)} %collective-permute-done.17), channel_id=1, source_target_pairs={{4,0},{8,4},{12,8},{16,12},{20,16},{24,20},{28,24},{32,28},{36,32}... | collective-permute-start | bytes 2752520 | tf_op jit(solution)/shard_map/ppermute | solution.py:16
  273.8 5.8 %collective-permute-start.21 = (bf16[2,256,896]{2,1,0:T(8,128)(2,1)}, bf16[2,256,896]{2,1,0:T(8,128)(2,1)}, u32[]{:S(2)}, u32[]{:S(2)}) collective-permute-start(bf16[2,256,896]{2,1,0:T(8,128)(2,1)} %collective-permute-done.19), channel_id=1, source_target_pairs={{4,0},{8,4},{12,8},{16,12},{20,16},{24,20},{28,24},{32,28},{36,32}... | collective-permute-start | bytes 2752520 | tf_op jit(solution)/shard_map/ppermute | solution.py:16
  290.8 5.9 %collective-permute-start.23 = (bf16[2,256,896]{2,1,0:T(8,128)(2,1)}, bf16[2,256,896]{2,1,0:T(8,128)(2,1)}, u32[]{:S(2)}, u32[]{:S(2)}) collective-permute-start(bf16[2,256,896]{2,1,0:T(8,128)(2,1)} %collective-permute-done.21), channel_id=1, source_target_pairs={{4,0},{8,4},{12,8},{16,12},{20,16},{24,20},{28,24},{32,28},{36,32}... | collective-permute-start | bytes 2752520 | tf_op jit(solution)/shard_map/ppermute | solution.py:16
  307.9 5.9 %collective-permute-start.25 = (bf16[2,256,896]{2,1,0:T(8,128)(2,1)}, bf16[2,256,896]{2,1,0:T(8,128)(2,1)}, u32[]{:S(2)}, u32[]{:S(2)}) collective-permute-start(bf16[2,256,896]{2,1,0:T(8,128)(2,1)} %collective-permute-done.23), channel_id=1, source_target_pairs={{4,0},{8,4},{12,8},{16,12},{20,16},{24,20},{28,24},{32,28},{36,32}... | collective-permute-start | bytes 2752520 | tf_op jit(solution)/shard_map/ppermute | solution.py:16
  318.2 7.6 %collective-permute-done.22 = bf16[4,256,896]{2,1,0:T(8,128)(2,1)} collective-permute-done((bf16[4,256,896]{2,1,0:T(8,128)(2,1)}, bf16[4,256,896]{2,1,0:T(8,128)(2,1)}, u32[]{:S(2)}, u32[]{:S(2)}) %collective-permute-start.22) | collective-permute-done | bytes 1835040 | tf_op jit(solution)/shard_map/ppermute | solution.py:16
  330.9 5.7 %collective-permute-start.27 = (bf16[2,256,896]{2,1,0:T(8,128)(2,1)}, bf16[2,256,896]{2,1,0:T(8,128)(2,1)}, u32[]{:S(2)}, u32[]{:S(2)}) collective-permute-start(bf16[2,256,896]{2,1,0:T(8,128)(2,1)} %collective-permute-done.25), channel_id=1, source_target_pairs={{4,0},{8,4},{12,8},{16,12},{20,16},{24,20},{28,24},{32,28},{36,32}... | collective-permute-start | bytes 2752520 | tf_op jit(solution)/shard_map/ppermute | solution.py:16
  347.4 5.3 %collective-permute-done.24 = bf16[4,256,896]{2,1,0:T(8,128)(2,1)} collective-permute-done((bf16[4,256,896]{2,1,0:T(8,128)(2,1)}, bf16[4,256,896]{2,1,0:T(8,128)(2,1)}, u32[]{:S(2)}, u32[]{:S(2)}) %collective-permute-start.24) | collective-permute-done | bytes 1835040 | tf_op jit(solution)/shard_map/ppermute | solution.py:16
  354.7 6.4 %fusion.154 = f32[256,896]{1,0:T(8,128)} fusion(bf16[256,3584]{1,0:T(8,128)(2,1)} %all-gather.2.cloned.1.call-done, bf16[3584,896]{1,0:T(8,128)(2,1)} %param.42), kind=kOutput, calls=%fused_computation.381 | convolution fusion | flops 1644167168 | bytes 9175040 | tf_op jit(solution)/shard_map/dot_general | solution.py:204
  372.8 6.9 %collective-permute-done.26 = bf16[4,256,896]{2,1,0:T(8,128)(2,1)} collective-permute-done((bf16[4,256,896]{2,1,0:T(8,128)(2,1)}, bf16[4,256,896]{2,1,0:T(8,128)(2,1)}, u32[]{:S(2)}, u32[]{:S(2)}) %collective-permute-start.26) | collective-permute-done | bytes 1835040 | tf_op jit(solution)/shard_map/ppermute | solution.py:16
  403.2 56.2 %while.2 = (s32[]{:T(128)}, bf16[4,256,224]{1,2,0:T(8,128)(2,1)}, s32[4]{0:T(128)S(1)}, bf16[256,896]{1,0:T(8,128)(2,1)S(1)}, bf16[7424,896]{1,0:T(8,128)(2,1)},...) while((s32[]{:T(128)}, bf16[4,256,224]{1,2,0:T(8,128)(2,1)}, ...), condition=%wide.region_30.31_spmd, body=%wide.region_27.30_spmd.sunk | while | flops 1718148608 | bytes 32561836 | solution.py:255
  410.9 6.6 %fusion.172 = bf16[4,256,224]{1,2,0:T(8,128)(2,1)} fusion(bf16[4,256,224]{1,2,0:T(8,128)(2,1)} %get-tuple-element.297, s32[]{:T(128)} %get-tuple-element.296, bf16[7424,896]{1,0:T(8,128)(2,1)} %get-tuple-element.313, s32[]{:T(128)S(6)} %select_n.233, f32[256,7424]{1,0:T(8,128)S(1)} %get-tuple-element.283, f32[256]{0:T(256)S(1)} %fusion.171, ...), kind=kOutput, calls=%fused_computation.11.clone.1 | convolution fusion | flops 857202688 | bytes 11520516 | tf_op jit(solution)/shard_map/while/body/eval_jaxpr/dot_general | solution.py:253
  418.8 5.3 %fusion.170 = (f32[256]{0:T(256)S(1)}, f32[256,7424]{1,0:T(8,128)S(1)}) fusion(pred[256,7424]{1,0:T(32,128)(4,1)S(1)} %get-tuple-element.312, bf16[7424,896]{1,0:T(8,128)(2,1)} %get-tuple-element.311, s32[]{:T(128)S(6)} %select_n.233, bf16[256,896]{1,0:T(8,128)(2,1)S(1)} %get-tuple-element.310), kind=kOutput, calls=%fused_computation.378.clone.1 | convolution fusion | flops 857145088 | bytes 13436928 | tf_op jit(solution)/shard_map/while/body/eval_jaxpr/dot_general | solution.py:244
  425.3 6.6 %fusion.172 = bf16[4,256,224]{1,2,0:T(8,128)(2,1)} fusion(bf16[4,256,224]{1,2,0:T(8,128)(2,1)} %get-tuple-element.297, s32[]{:T(128)} %get-tuple-element.296, bf16[7424,896]{1,0:T(8,128)(2,1)} %get-tuple-element.313, s32[]{:T(128)S(6)} %select_n.233, f32[256,7424]{1,0:T(8,128)S(1)} %get-tuple-element.283, f32[256]{0:T(256)S(1)} %fusion.171, ...), kind=kOutput, calls=%fused_computation.11.clone.1 | convolution fusion | flops 857202688 | bytes 11520516 | tf_op jit(solution)/shard_map/while/body/eval_jaxpr/dot_general | solution.py:253
  433.1 5.3 %fusion.170 = (f32[256]{0:T(256)S(1)}, f32[256,7424]{1,0:T(8,128)S(1)}) fusion(pred[256,7424]{1,0:T(32,128)(4,1)S(1)} %get-tuple-element.312, bf16[7424,896]{1,0:T(8,128)(2,1)} %get-tuple-element.311, s32[]{:T(128)S(6)} %select_n.233, bf16[256,896]{1,0:T(8,128)(2,1)S(1)} %get-tuple-element.310), kind=kOutput, calls=%fused_computation.378.clone.1 | convolution fusion | flops 857145088 | bytes 13436928 | tf_op jit(solution)/shard_map/while/body/eval_jaxpr/dot_general | solution.py:244
  439.6 6.6 %fusion.172 = bf16[4,256,224]{1,2,0:T(8,128)(2,1)} fusion(bf16[4,256,224]{1,2,0:T(8,128)(2,1)} %get-tuple-element.297, s32[]{:T(128)} %get-tuple-element.296, bf16[7424,896]{1,0:T(8,128)(2,1)} %get-tuple-element.313, s32[]{:T(128)S(6)} %select_n.233, f32[256,7424]{1,0:T(8,128)S(1)} %get-tuple-element.283, f32[256]{0:T(256)S(1)} %fusion.171, ...), kind=kOutput, calls=%fused_computation.11.clone.1 | convolution fusion | flops 857202688 | bytes 11520516 | tf_op jit(solution)/shard_map/while/body/eval_jaxpr/dot_general | solution.py:253
  453.4 6.0 %fusion.172 = bf16[4,256,224]{1,2,0:T(8,128)(2,1)} fusion(bf16[4,256,224]{1,2,0:T(8,128)(2,1)} %get-tuple-element.297, s32[]{:T(128)} %get-tuple-element.296, bf16[7424,896]{1,0:T(8,128)(2,1)} %get-tuple-element.313, s32[]{:T(128)S(6)} %select_n.233, f32[256,7424]{1,0:T(8,128)S(1)} %get-tuple-element.283, f32[256]{0:T(256)S(1)} %fusion.171, ...), kind=kOutput, calls=%fused_computation.11.clone.1 | convolution fusion | flops 857202688 | bytes 11520516 | tf_op jit(solution)/shard_map/while/body/eval_jaxpr/dot_general | solution.py:253
  (283 shorter events, 203.8 us)
Async XLA Ops:
  7.2 353.9 %copy-start = (bf16[3584,128]{1,0:T(8,128)(2,1)S(1)}, bf16[3584,128]{1,0:T(8,128)(2,1)}, u32[]{:S(2)}) copy-start(bf16[3584,128]{1,0:T(8,128)(2,1)} %param.43) | copy-start | bytes 2752516
  7.2 289.5 %reduce-scatter.2.cloned.1.call-start = ((), (), s32[]{:S(2)}) async-start(), calls=%async_computation.1 | async-start | bytes 4587520 | tf_op jit(solution)/shard_map/reduce_scatter | solution.py:190
  10.3 116.7 %collective-permute-start.10 = (bf16[4,256,896]{2,1,0:T(8,128)(2,1)}, bf16[4,256,896]{2,1,0:T(8,128)(2,1)}, u32[]{:S(2)}, u32[]{:S(2)}) collective-permute-start(bf16[4,256,896]{2,1,0:T(8,128)(2,1)} %pad_maximum_fusion), channel_id=1, source_target_pairs={{0,4},{4,8},{8,12},{12,16},{16,20},{20,24},{24,28},{28,32},{32,36}... | collective-permute-start | bytes 5505032 | tf_op jit(solution)/shard_map/ppermute | solution.py:16
  12.9 39.7 %collective-permute-start = (bf16[3,896]{1,0:T(4,128)(2,1)S(1)}, bf16[3,896]{1,0:T(4,128)(2,1)}, u32[]{:S(2)}, u32[]{:S(2)}) collective-permute-start(bf16[3,896]{1,0:T(4,128)(2,1)S(1)} %slice.293), channel_id=1, source_target_pairs={{0,4},{4,8},{8,12},{12,16},{16,20},{20,24},{24,28},{28,32},{32,36}... | collective-permute-start | bytes 16136 | tf_op jit(solution)/shard_map/ppermute | solution.py:16
  17.7 33.8 %collective-permute-start.1 = (bf16[3,128]{0,1:T(8,128)(2,1)S(1)}, bf16[3,128]{0,1:T(8,128)(2,1)}, u32[]{:S(2)}, u32[]{:S(2)}) collective-permute-start(bf16[3,128]{0,1:T(8,128)(2,1)S(1)} %copy.92), channel_id=1, source_target_pairs={{0,4},{4,8},{8,12},{12,16},{16,20},{20,24},{24,28},{28,32},{32,36}... | collective-permute-start | bytes 2312 | tf_op jit(solution)/shard_map/ppermute | solution.py:16
  28.4 47.4 %collective-permute-start.2 = (f32[14]{0:T(128)S(1)}, f32[14]{0:T(128)}, u32[]{:S(2)}, u32[]{:S(2)}) collective-permute-start(f32[14]{0:T(128)S(1)} %get-tuple-element.112), channel_id=1, source_target_pairs={{0,4},{4,8},{8,12},{12,16},{16,20},{20,24},{24,28},{28,32},{32,36}... | collective-permute-start | bytes 176 | tf_op jit(solution)/shard_map/ppermute | solution.py:16
  60.4 11.9 %collective-permute-start.5 = (f32[14,64,64]{2,1,0:T(8,128)S(1)}, f32[14,64,64]{2,1,0:T(8,128)S(1)}, u32[]{:S(2)}, u32[]{:S(2)}) collective-permute-start(f32[14,64,64]{2,1,0:T(8,128)S(1)} %convolution_add_fusion.1), channel_id=1, source_target_pairs={{0,4},{4,8},{8,12},{12,16},{16,20},{20,24},{24,28},{28,32},{32,36}... | collective-permute-start | bytes 688136 | tf_op jit(solution)/shard_map/ppermute | solution.py:16
  73.1 21.7 %collective-permute-start.6 = (f32[14,64,64]{2,1,0:T(8,128)}, f32[14,64,64]{2,1,0:T(8,128)}, u32[]{:S(2)}, u32[]{:S(2)}) collective-permute-start(f32[14,64,64]{2,1,0:T(8,128)} %multiply_add_fusion.3), channel_id=1, source_target_pairs={{0,8},{4,12},{8,16},{12,20},{16,24},{20,28},{24,32},{28,36},{32,40... | collective-permute-start | bytes 688136 | tf_op jit(solution)/shard_map/ppermute | solution.py:16
  76.4 10.7 %collective-permute-start.3 = (f32[14]{0:T(128)S(1)}, f32[14]{0:T(128)S(1)}, u32[]{:S(2)}, u32[]{:S(2)}) collective-permute-start(f32[14]{0:T(128)S(1)} %mul.379), channel_id=1, source_target_pairs={{0,8},{4,12},{8,16},{12,20},{16,24},{20,28},{24,32},{28,36},{32,40... | collective-permute-start | bytes 176 | tf_op jit(solution)/shard_map/ppermute | solution.py:16
  87.0 7.8 %collective-permute-start.4 = (f32[14]{0:T(128)S(1)}, f32[14]{0:T(128)S(1)}, u32[]{:S(2)}, u32[]{:S(2)}) collective-permute-start(f32[14]{0:T(128)S(1)} %mul.380), channel_id=1, source_target_pairs={{0,16},{4,20},{8,24},{12,28},{16,32},{20,36},{24,40},{28,44},{32,4... | collective-permute-start | bytes 176 | tf_op jit(solution)/shard_map/ppermute | solution.py:16
  96.1 15.3 %collective-permute-start.7 = (f32[14,64,64]{2,1,0:T(8,128)S(1)}, f32[14,64,64]{2,1,0:T(8,128)S(1)}, u32[]{:S(2)}, u32[]{:S(2)}) collective-permute-start(f32[14,64,64]{2,1,0:T(8,128)S(1)} %multiply_add_fusion.2), channel_id=1, source_target_pairs={{0,16},{4,20},{8,24},{12,28},{16,32},{20,36},{24,40},{28,44},{32,4... | collective-permute-start | bytes 688136 | tf_op jit(solution)/shard_map/ppermute | solution.py:16
  111.5 10.4 %collective-permute-start.8 = (f32[14,64,64]{2,1,0:T(8,128)S(1)}, f32[14,64,64]{2,1,0:T(8,128)S(1)}, u32[]{:S(2)}, u32[]{:S(2)}) collective-permute-start(f32[14,64,64]{2,1,0:T(8,128)S(1)} %multiply_add_fusion.1), channel_id=1, source_target_pairs={{0,32},{4,36},{8,40},{12,44},{16,48},{20,52},{24,56},{28,60},{32,6... | collective-permute-start | bytes 688136 | tf_op jit(solution)/shard_map/ppermute | solution.py:16
  122.0 11.9 %collective-permute-start.9 = (f32[14,64,64]{2,1,0:T(8,128)S(1)}, f32[14,64,64]{2,1,0:T(8,128)S(1)}, u32[]{:S(2)}, u32[]{:S(2)}) collective-permute-start(f32[14,64,64]{2,1,0:T(8,128)S(1)} %multiply_add_fusion), channel_id=1, source_target_pairs={{0,4},{4,8},{8,12},{12,16},{16,20},{20,24},{24,28},{28,32},{32,36}... | collective-permute-start | bytes 688136 | tf_op jit(solution)/shard_map/ppermute | solution.py:16
  127.0 48.3 %collective-permute-start.12 = (bf16[4,256,896]{2,1,0:T(8,128)(2,1)}, bf16[4,256,896]{2,1,0:T(8,128)(2,1)}, u32[]{:S(2)}, u32[]{:S(2)}) collective-permute-start(bf16[4,256,896]{2,1,0:T(8,128)(2,1)} %collective-permute-done.10), channel_id=1, source_target_pairs={{0,4},{4,8},{8,12},{12,16},{16,20},{20,24},{24,28},{28,32},{32,36}... | collective-permute-start | bytes 5505032 | tf_op jit(solution)/shard_map/ppermute | solution.py:16
  175.3 125.5 %copy-start.22 = (f32[3584]{0:T(1024)S(1)}, f32[3584]{0:T(1024)}, u32[]{:S(2)}) copy-start(f32[3584]{0:T(1024)} %param.41) | copy-start | bytes 43012
  175.3 179.4 %all-gather.2.cloned.1.call-start = ((), (), s32[]{:S(2)}) async-start(), calls=%async_computation.2 | async-start | bytes 2293760 | tf_op jit(solution)/shard_map/all_gather | solution.py:201
  175.3 26.9 %collective-permute-start.14 = (bf16[4,256,896]{2,1,0:T(8,128)(2,1)}, bf16[4,256,896]{2,1,0:T(8,128)(2,1)S(1)}, u32[]{:S(2)}, u32[]{:S(2)}) collective-permute-start(bf16[4,256,896]{2,1,0:T(8,128)(2,1)} %collective-permute-done.12), channel_id=1, source_target_pairs={{0,4},{4,8},{8,12},{12,16},{16,20},{20,24},{24,28},{28,32},{32,36}... | collective-permute-start | bytes 5505032 | tf_op jit(solution)/shard_map/ppermute | solution.py:16
  177.4 28.0 %collective-permute-start.11 = (bf16[2,256,896]{2,1,0:T(8,128)(2,1)S(1)}, bf16[2,256,896]{2,1,0:T(8,128)(2,1)S(1)}, u32[]{:S(2)}, u32[]{:S(2)}) collective-permute-start(bf16[2,256,896]{2,1,0:T(8,128)(2,1)S(1)} %pad_maximum_fusion.1), channel_id=1, source_target_pairs={{4,0},{8,4},{12,8},{16,12},{20,16},{24,20},{28,24},{32,28},{36,32}... | collective-permute-start | bytes 2752520 | tf_op jit(solution)/shard_map/ppermute | solution.py:16
  203.4 26.6 %collective-permute-start.16 = (bf16[4,256,896]{2,1,0:T(8,128)(2,1)S(1)}, bf16[4,256,896]{2,1,0:T(8,128)(2,1)S(1)}, u32[]{:S(2)}, u32[]{:S(2)}) collective-permute-start(bf16[4,256,896]{2,1,0:T(8,128)(2,1)S(1)} %collective-permute-done.14), channel_id=1, source_target_pairs={{0,4},{4,8},{8,12},{12,16},{16,20},{20,24},{24,28},{28,32},{32,36}... | collective-permute-start | bytes 5505032 | tf_op jit(solution)/shard_map/ppermute | solution.py:16
  205.4 16.6 %collective-permute-start.13 = (bf16[2,256,896]{2,1,0:T(8,128)(2,1)S(1)}, bf16[2,256,896]{2,1,0:T(8,128)(2,1)S(1)}, u32[]{:S(2)}, u32[]{:S(2)}) collective-permute-start(bf16[2,256,896]{2,1,0:T(8,128)(2,1)S(1)} %collective-permute-done.11), channel_id=1, source_target_pairs={{4,0},{8,4},{12,8},{16,12},{20,16},{24,20},{28,24},{32,28},{36,32}... | collective-permute-start | bytes 2752520 | tf_op jit(solution)/shard_map/ppermute | solution.py:16
  222.0 16.8 %collective-permute-start.15 = (bf16[2,256,896]{2,1,0:T(8,128)(2,1)S(1)}, bf16[2,256,896]{2,1,0:T(8,128)(2,1)S(1)}, u32[]{:S(2)}, u32[]{:S(2)}) collective-permute-start(bf16[2,256,896]{2,1,0:T(8,128)(2,1)S(1)} %collective-permute-done.13), channel_id=1, source_target_pairs={{4,0},{8,4},{12,8},{16,12},{20,16},{24,20},{28,24},{32,28},{36,32}... | collective-permute-start | bytes 2752520 | tf_op jit(solution)/shard_map/ppermute | solution.py:16
  231.3 40.6 %collective-permute-start.18 = (bf16[4,256,896]{2,1,0:T(8,128)(2,1)S(1)}, bf16[4,256,896]{2,1,0:T(8,128)(2,1)}, u32[]{:S(2)}, u32[]{:S(2)}) collective-permute-start(bf16[4,256,896]{2,1,0:T(8,128)(2,1)S(1)} %collective-permute-done.16), channel_id=1, source_target_pairs={{0,4},{4,8},{8,12},{12,16},{16,20},{20,24},{24,28},{28,32},{32,36}... | collective-permute-start | bytes 5505032 | tf_op jit(solution)/shard_map/ppermute | solution.py:16
  238.8 16.8 %collective-permute-start.17 = (bf16[2,256,896]{2,1,0:T(8,128)(2,1)S(1)}, bf16[2,256,896]{2,1,0:T(8,128)(2,1)S(1)}, u32[]{:S(2)}, u32[]{:S(2)}) collective-permute-start(bf16[2,256,896]{2,1,0:T(8,128)(2,1)S(1)} %collective-permute-done.15), channel_id=1, source_target_pairs={{4,0},{8,4},{12,8},{16,12},{20,16},{24,20},{28,24},{32,28},{36,32}... | collective-permute-start | bytes 2752520 | tf_op jit(solution)/shard_map/ppermute | solution.py:16
  255.6 18.1 %collective-permute-start.19 = (bf16[2,256,896]{2,1,0:T(8,128)(2,1)S(1)}, bf16[2,256,896]{2,1,0:T(8,128)(2,1)}, u32[]{:S(2)}, u32[]{:S(2)}) collective-permute-start(bf16[2,256,896]{2,1,0:T(8,128)(2,1)S(1)} %collective-permute-done.17), channel_id=1, source_target_pairs={{4,0},{8,4},{12,8},{16,12},{20,16},{24,20},{28,24},{32,28},{36,32}... | collective-permute-start | bytes 2752520 | tf_op jit(solution)/shard_map/ppermute | solution.py:16
  271.9 27.0 %collective-permute-start.20 = (bf16[4,256,896]{2,1,0:T(8,128)(2,1)}, bf16[4,256,896]{2,1,0:T(8,128)(2,1)}, u32[]{:S(2)}, u32[]{:S(2)}) collective-permute-start(bf16[4,256,896]{2,1,0:T(8,128)(2,1)} %collective-permute-done.18), channel_id=1, source_target_pairs={{0,4},{4,8},{8,12},{12,16},{16,20},{20,24},{24,28},{28,32},{32,36}... | collective-permute-start | bytes 5505032 | tf_op jit(solution)/shard_map/ppermute | solution.py:16
  273.8 17.0 %collective-permute-start.21 = (bf16[2,256,896]{2,1,0:T(8,128)(2,1)}, bf16[2,256,896]{2,1,0:T(8,128)(2,1)}, u32[]{:S(2)}, u32[]{:S(2)}) collective-permute-start(bf16[2,256,896]{2,1,0:T(8,128)(2,1)} %collective-permute-done.19), channel_id=1, source_target_pairs={{4,0},{8,4},{12,8},{16,12},{20,16},{24,20},{28,24},{32,28},{36,32}... | collective-permute-start | bytes 2752520 | tf_op jit(solution)/shard_map/ppermute | solution.py:16
  290.8 17.1 %collective-permute-start.23 = (bf16[2,256,896]{2,1,0:T(8,128)(2,1)}, bf16[2,256,896]{2,1,0:T(8,128)(2,1)}, u32[]{:S(2)}, u32[]{:S(2)}) collective-permute-start(bf16[2,256,896]{2,1,0:T(8,128)(2,1)} %collective-permute-done.21), channel_id=1, source_target_pairs={{4,0},{8,4},{12,8},{16,12},{20,16},{24,20},{28,24},{32,28},{36,32}... | collective-permute-start | bytes 2752520 | tf_op jit(solution)/shard_map/ppermute | solution.py:16
  298.8 27.0 %collective-permute-start.22 = (bf16[4,256,896]{2,1,0:T(8,128)(2,1)}, bf16[4,256,896]{2,1,0:T(8,128)(2,1)}, u32[]{:S(2)}, u32[]{:S(2)}) collective-permute-start(bf16[4,256,896]{2,1,0:T(8,128)(2,1)} %collective-permute-done.20), channel_id=1, source_target_pairs={{0,4},{4,8},{8,12},{12,16},{16,20},{20,24},{24,28},{28,32},{32,36}... | collective-permute-start | bytes 5505032 | tf_op jit(solution)/shard_map/ppermute | solution.py:16
  307.9 23.0 %collective-permute-start.25 = (bf16[2,256,896]{2,1,0:T(8,128)(2,1)}, bf16[2,256,896]{2,1,0:T(8,128)(2,1)}, u32[]{:S(2)}, u32[]{:S(2)}) collective-permute-start(bf16[2,256,896]{2,1,0:T(8,128)(2,1)} %collective-permute-done.23), channel_id=1, source_target_pairs={{4,0},{8,4},{12,8},{16,12},{20,16},{24,20},{28,24},{32,28},{36,32}... | collective-permute-start | bytes 2752520 | tf_op jit(solution)/shard_map/ppermute | solution.py:16
  325.8 27.0 %collective-permute-start.24 = (bf16[4,256,896]{2,1,0:T(8,128)(2,1)}, bf16[4,256,896]{2,1,0:T(8,128)(2,1)}, u32[]{:S(2)}, u32[]{:S(2)}) collective-permute-start(bf16[4,256,896]{2,1,0:T(8,128)(2,1)} %collective-permute-done.22), channel_id=1, source_target_pairs={{0,4},{4,8},{8,12},{12,16},{16,20},{20,24},{24,28},{28,32},{32,36}... | collective-permute-start | bytes 5505032 | tf_op jit(solution)/shard_map/ppermute | solution.py:16
  330.9 51.0 %collective-permute-start.27 = (bf16[2,256,896]{2,1,0:T(8,128)(2,1)}, bf16[2,256,896]{2,1,0:T(8,128)(2,1)}, u32[]{:S(2)}, u32[]{:S(2)}) collective-permute-start(bf16[2,256,896]{2,1,0:T(8,128)(2,1)} %collective-permute-done.25), channel_id=1, source_target_pairs={{4,0},{8,4},{12,8},{16,12},{20,16},{24,20},{28,24},{32,28},{36,32}... | collective-permute-start | bytes 2752520 | tf_op jit(solution)/shard_map/ppermute | solution.py:16
  352.7 27.0 %collective-permute-start.26 = (bf16[4,256,896]{2,1,0:T(8,128)(2,1)}, bf16[4,256,896]{2,1,0:T(8,128)(2,1)}, u32[]{:S(2)}, u32[]{:S(2)}) collective-permute-start(bf16[4,256,896]{2,1,0:T(8,128)(2,1)} %collective-permute-done.24), channel_id=1, source_target_pairs={{0,4},{4,8},{8,12},{12,16},{16,20},{20,24},{24,28},{28,32},{32,36}... | collective-permute-start | bytes 5505032 | tf_op jit(solution)/shard_map/ppermute | solution.py:16
  (26 other events, 538.9 us)
Sparse Core Ops, SparseCore 0:
  175.4 38.7 reduce-scatter.1
  301.9 28.2 all-gather.1

commit v3 on v1

--- a/solution.py
+++ b/solution.py
@@ -82,6 +82,33 @@
     seq_count = lax.axis_size("seq")
     reach = seq_count // 4 + 1
     first = seq_index * length
+    long_hop = seq_count // 4
+    behind_pieces = [jnp.stack([cache_keys, cache_values, new_keys, new_values])] * (reach + 1)
+    forward_pieces = [jnp.stack([cache_keys, cache_values])] * (reach + 1)
+    relay_steps = []
+    for distance in range(1, long_hop):
+        relay_steps.append([(distance, distance - 1, 1)])
+    for distance in range(long_hop, reach + 1):
+        relay_steps[distance - long_hop].append((distance, distance - long_hop, long_hop))
+
+    def advance(values):
+        if not relay_steps:
+            return values
+        moves = relay_steps.pop(0)
+        sent = []
+        for distance, source, steps in moves:
+            sent.append(
+                (
+                    shifted_2(behind_pieces[source], "seq", steps),
+                    shifted_2(forward_pieces[source], "seq", -steps),
+                )
+            )
+        sent, values = lax.optimization_barrier((sent, values))
+        for (distance, _, _), (behind, forward) in zip(moves, sent):
+            behind_pieces[distance] = behind
+            forward_pieces[distance] = forward
+        return values
+
     local_index = first + jnp.arange(length, dtype=jnp.int32)
     segment, begin, valid, onehot = locate(lengths, local_index)
     position = local_index - begin
@@ -90,6 +117,7 @@
     )
     x_conv = convolve(x_in, x_border, conv_x_cache, conv_x_weight, position, onehot)
     bc_conv = convolve(bc_in, bc_border, conv_bc_cache, conv_bc_weight, position, onehot)
+    x_conv, bc_conv = advance((x_conv, bc_conv))
     heads = dt_bias.shape[0]
     state_size = bc_in.shape[1] // 2
     head_size = x_in.shape[1] // heads
@@ -149,14 +177,15 @@
     )
     chain_decay = jnp.where(starts_here, jnp.zeros_like(whole_decay), whole_decay)
 
-    scan_decay, scan_state = chain_decay, chain_state
+    scan_decay, scan_state = advance((chain_decay, chain_state))
     distance = 1
     while distance <= reach and distance < seq_count:
         prior_decay, prior_state = shifted_2((scan_decay, scan_state), "seq", distance)
         scan_state = scan_decay[:, None, None] * prior_state + scan_state
         scan_decay = scan_decay * prior_decay
+        scan_decay, scan_state = advance((scan_decay, scan_state))
         distance *= 2
-    carried = shifted_2(scan_state, "seq", 1)
+    carried = advance(shifted_2(scan_state, "seq", 1))
     continuing = position[0] > 0
     replace = (jnp.arange(prompts, dtype=jnp.int32) == segment[0]) & continuing
     initial = jnp.where(replace[:, None, None, None], carried[None], ssm_cache)
@@ -179,6 +208,7 @@
     normed = (gated * lax.rsqrt(squares / width + EPS)[:, None] * norm_gain[None, :]).astype(
         jnp.bfloat16
     )
+    normed = advance(normed)
     summed = lax.psum_scatter(
         jnp.dot(normed, out_weight, preferred_element_type=jnp.float32),
         "tp",
@@ -208,11 +238,13 @@
 
     cache_pieces = [(cache_keys, cache_values, 0)]
     new_pieces = [(new_keys, new_values, 0)]
+    while relay_steps:
+        advance(())
     for distance in range(1, reach + 1):
-        behind = shifted_2((cache_keys, cache_values, new_keys, new_values), "seq", distance)
+        behind = behind_pieces[distance]
         cache_pieces.append((behind[0], behind[1], -distance))
         new_pieces.append((behind[2], behind[3], -distance))
-        forward = shifted_2((cache_keys, cache_values), "seq", -distance)
+        forward = forward_pieces[distance]
         cache_pieces.append((forward[0], forward[1], distance))
     all_keys = jnp.concatenate(
         [entry[0] for entry in cache_pieces] + [entry[0] for entry in new_pieces], axis=0

time: 702 us -> 516 us (0.74)
  the two profiles are of different devices: /device:TPU:16 before, /device:TPU:1 now
where the time goes in v3:
time: 516 us; the launch traced here: 506 us
  starting transfers between devices  191 us (37%)
  local copies, waits for them, and re-layouts  89.6 us (17%)
  matrix products  79.5 us (15%)
  waiting for transfers between devices  78.9 us (15%)
  other arithmetic  36.4 us (7%)
  between operations  19 us (4%)
  blocking collectives  8.68 us (2%)
    ppermute x28, starting transfers between devices, shifted_2(): lax.ppermute(value, axis, [(source, source + steps) for source in range(i...  191 us
    unnamed x95, local copies, waits for them, and re-layouts  57.1 us
    ppermute x28, waiting for transfers between devices, shifted_2(): lax.ppermute(value, axis, [(source, source + steps) for source in range(i...  51.1 us
    dot_general x4, matrix products, attend(): jnp.dot(probs, value_head, preferred_element_type=jnp.float32)  25.7 us
    dot_general x4, matrix products, attend(): lax.dot_general(query_head, key_head, (((1,), (1,)), ((), ())), preferred...  20.6 us
    reduce_scatter x1, waiting for transfers between devices, per_device(): lax.psum_scatter(jnp.dot(normed, out_weight, preferred_element_type=jnp.f...  19.4 us
  transfers between devices with their start and end apart: 30, of which 12 were waited for; matrix products, arithmetic and copies ran while one was open for 21% of the time, Pallas kernels for 0%

profile of v3, /device:TPU:1, one launch (start us, length us, event | category | flops | bytes accessed | tf_op | source)
XLA Modules:
  0.0 505.8 jit_solution(13095270637040389307)
XLA Ops:
  10.3 4.9 collective-permute-start
  60.3 31.2 %collective-permute-start.8 = (bf16[4,256,896]{2,1,0:T(8,128)(2,1)}, bf16[4,256,896]{2,1,0:T(8,128)(2,1)}, u32[]{:S(2)}, u32[]{:S(2)}) collective-permute-start(bf16[4,256,896]{2,1,0:T(8,128)(2,1)} %collective-permute-done), channel_id=1, source_target_pairs={{0,32},{4,36},{8,40},{12,44},{16,48},{20,52},{24,56},{28,60},{32,6... | collective-permute-start | bytes 5505032 | tf_op jit(solution)/shard_map/ppermute | solution.py:16
  95.7 6.7 %collective-permute-start.7 = (bf16[2,256,896]{2,1,0:T(8,128)(2,1)}, bf16[2,256,896]{2,1,0:T(8,128)(2,1)}, u32[]{:S(2)}, u32[]{:S(2)}) collective-permute-start(bf16[2,256,896]{2,1,0:T(8,128)(2,1)} %collective-permute-done.1), channel_id=1, source_target_pairs={{4,0},{8,4},{12,8},{16,12},{20,16},{24,20},{28,24},{32,28},{36,32}... | collective-permute-start | bytes 2752520 | tf_op jit(solution)/shard_map/ppermute | solution.py:16
  110.8 14.2 %collective-permute-done.9 = bf16[2,256,896]{2,1,0:T(8,128)(2,1)} collective-permute-done((bf16[2,256,896]{2,1,0:T(8,128)(2,1)}, bf16[2,256,896]{2,1,0:T(8,128)(2,1)}, u32[]{:S(2)}, u32[]{:S(2)}) %collective-permute-start.9) | collective-permute-done | bytes 917536 | tf_op jit(solution)/shard_map/ppermute | solution.py:16
  128.4 13.3 %collective-permute-start.11 = (bf16[2,256,896]{2,1,0:T(8,128)(2,1)}, bf16[2,256,896]{2,1,0:T(8,128)(2,1)S(1)}, u32[]{:S(2)}, u32[]{:S(2)}) collective-permute-start(bf16[2,256,896]{2,1,0:T(8,128)(2,1)} %collective-permute-done.7), channel_id=1, source_target_pairs={{4,0},{8,4},{12,8},{16,12},{20,16},{24,20},{28,24},{32,28},{36,32}... | collective-permute-start | bytes 2752520 | tf_op jit(solution)/shard_map/ppermute | solution.py:16
  146.4 6.2 %collective-permute-done.12 = f32[14]{0:T(128)S(1)} collective-permute-done((f32[14]{0:T(128)S(1)}, f32[14]{0:T(128)S(1)}, u32[]{:S(2)}, u32[]{:S(2)}) %collective-permute-start.12) | collective-permute-done | bytes 88 | tf_op jit(solution)/shard_map/ppermute | solution.py:16
  160.3 13.1 %collective-permute-start.17 = (f32[14,64,64]{2,1,0:T(8,128)S(1)}, f32[14,64,64]{2,1,0:T(8,128)S(1)}, u32[]{:S(2)}, u32[]{:S(2)}) collective-permute-start(f32[14,64,64]{2,1,0:T(8,128)S(1)} %multiply_add_fusion.3), channel_id=1, source_target_pairs={{0,8},{4,12},{8,16},{12,20},{16,24},{20,28},{24,32},{28,36},{32,40... | collective-permute-start | bytes 688136 | tf_op jit(solution)/shard_map/ppermute | solution.py:16
  173.5 8.6 %collective-permute-start.16 = (f32[14]{0:T(128)S(1)}, f32[14]{0:T(128)S(1)}, u32[]{:S(2)}, u32[]{:S(2)}) collective-permute-start(f32[14]{0:T(128)S(1)} %mul.385), channel_id=1, source_target_pairs={{0,8},{4,12},{8,16},{12,20},{16,24},{20,28},{24,32},{28,36},{32,40... | collective-permute-start | bytes 176 | tf_op jit(solution)/shard_map/ppermute | solution.py:16
  187.4 9.0 %collective-permute-start.18 = (bf16[4,256,896]{2,1,0:T(8,128)(2,1)S(1)}, bf16[4,256,896]{2,1,0:T(8,128)(2,1)S(1)}, u32[]{:S(2)}, u32[]{:S(2)}) collective-permute-start(bf16[4,256,896]{2,1,0:T(8,128)(2,1)S(1)} %collective-permute-done.14), channel_id=1, source_target_pairs={{0,4},{4,8},{8,12},{12,16},{16,20},{20,24},{24,28},{28,32},{32,36}... | collective-permute-start | bytes 5505032 | tf_op jit(solution)/shard_map/ppermute | solution.py:16
  199.6 17.8 %collective-permute-start.21 = (f32[14,64,64]{2,1,0:T(8,128)S(1)}, f32[14,64,64]{2,1,0:T(8,128)S(1)}, u32[]{:S(2)}, u32[]{:S(2)}) collective-permute-start(f32[14,64,64]{2,1,0:T(8,128)S(1)} %multiply_add_fusion.2), channel_id=1, source_target_pairs={{0,16},{4,20},{8,24},{12,28},{16,32},{20,36},{24,40},{28,44},{32,4... | collective-permute-start | bytes 688136 | tf_op jit(solution)/shard_map/ppermute | solution.py:16
  218.1 15.3 %collective-permute-start.20 = (f32[14]{0:T(128)S(1)}, f32[14]{0:T(128)S(1)}, u32[]{:S(2)}, u32[]{:S(2)}) collective-permute-start(f32[14]{0:T(128)S(1)} %mul.388), channel_id=1, source_target_pairs={{0,16},{4,20},{8,24},{12,28},{16,32},{20,36},{24,40},{28,44},{32,4... | collective-permute-start | bytes 176 | tf_op jit(solution)/shard_map/ppermute | solution.py:16
  234.3 14.3 %collective-permute-start.22 = (bf16[4,256,896]{2,1,0:T(8,128)(2,1)S(1)}, bf16[4,256,896]{2,1,0:T(8,128)(2,1)}, u32[]{:S(2)}, u32[]{:S(2)}) collective-permute-start(bf16[4,256,896]{2,1,0:T(8,128)(2,1)S(1)} %collective-permute-done.18), channel_id=1, source_target_pairs={{0,4},{4,8},{8,12},{12,16},{16,20},{20,24},{24,28},{28,32},{32,36}... | collective-permute-start | bytes 5505032 | tf_op jit(solution)/shard_map/ppermute | solution.py:16
  251.4 8.5 %collective-permute-start.24 = (f32[14,64,64]{2,1,0:T(8,128)S(1)}, f32[14,64,64]{2,1,0:T(8,128)S(1)}, u32[]{:S(2)}, u32[]{:S(2)}) collective-permute-start(f32[14,64,64]{2,1,0:T(8,128)S(1)} %multiply_add_fusion.1), channel_id=1, source_target_pairs={{0,32},{4,36},{8,40},{12,44},{16,48},{20,52},{24,56},{28,60},{32,6... | collective-permute-start | bytes 688136 | tf_op jit(solution)/shard_map/ppermute | solution.py:16
  260.2 5.0 collective-permute-done.24
  268.8 9.9 %collective-permute-start.25 = (bf16[4,256,896]{2,1,0:T(8,128)(2,1)}, bf16[4,256,896]{2,1,0:T(8,128)(2,1)}, u32[]{:S(2)}, u32[]{:S(2)}) collective-permute-start(bf16[4,256,896]{2,1,0:T(8,128)(2,1)} %collective-permute-done.22), channel_id=1, source_target_pairs={{0,4},{4,8},{8,12},{12,16},{16,20},{20,24},{24,28},{28,32},{32,36}... | collective-permute-start | bytes 5505032 | tf_op jit(solution)/shard_map/ppermute | solution.py:16
  294.2 9.8 %collective-permute-done.27 = f32[14,64,64]{2,1,0:T(8,128)S(1)} collective-permute-done((f32[14,64,64]{2,1,0:T(8,128)S(1)}, f32[14,64,64]{2,1,0:T(8,128)S(1)}, u32[]{:S(2)}, u32[]{:S(2)}) %collective-permute-start.27) | collective-permute-done | bytes 229408 | tf_op jit(solution)/shard_map/ppermute | solution.py:16
  308.1 8.4 %copy.89 = f32[16,64,14,64]{1,0,3,2:T(8,128)} copy(f32[16,64,14,64]{1,3,2,0:T(8,128)S(1)} %select_bitcast_fusion) | data formatting | bytes 7340032 | tf_op jit(solution)/shard_map/transpose | solution.py:195
  316.4 7.4 %reshape.575 = f32[1024,896]{0,1:T(8,128)} reshape(f32[16,64,14,64]{1,0,3,2:T(8,128)} %copy.89) | data formatting | bytes 7340032 | tf_op jit(solution)/shard_map/reshape | solution.py:195
  327.7 8.7 %psum.7 = f32[256]{0:T(256)S(1)} all-reduce(f32[256]{0:T(256)S(1)} %get-tuple-element.258), channel_id=1, replica_groups=mesh['seq'=32,'tp'=4] {'tp'}, use_global_device_ids=true, to_apply=%region_6.7 | all-reduce | flops 256 | bytes 2048 | tf_op jit(solution)/shard_map/psum | solution.py:206
  336.6 6.9 %fusion.99 = f32[256,3584]{1,0:T(8,128)} fusion(bf16[256,896]{0,1:T(8,128)(2,1)S(1)} %fusion.41, bf16[896,3584]{1,0:T(8,128)(2,1)} %param.40), kind=kOutput, calls=%fused_computation.324 | convolution fusion | flops 1644167168 | bytes 10551296 | tf_op jit(solution)/shard_map/dot_general | solution.py:213
  379.9 19.4 %reduce-scatter.2.cloned.1.call-done = f32[64,3584]{1,0:T(8,128)} async-done(((f32[256,3584]{1,0:T(8,128)}), f32[64,3584]{1,0:T(8,128)}) %reduce-scatter.2.cloned.1.call-update) | async-done | bytes 917520 | tf_op jit(solution)/shard_map/reduce_scatter | solution.py:212
  422.6 8.4 %all-gather.2.cloned.1.call-done = bf16[256,3584]{1,0:T(8,128)(2,1)} async-done(((bf16[64,3584]{1,0:T(8,128)(2,1)}), bf16[256,3584]{1,0:T(8,128)(2,1)}) %all-gather.2.cloned.1.call-update) | async-done | bytes 1835024 | tf_op jit(solution)/shard_map/all_gather | solution.py:223
  431.0 6.4 %fusion.100 = f32[256,896]{1,0:T(8,128)} fusion(bf16[256,3584]{1,0:T(8,128)(2,1)} %all-gather.2.cloned.1.call-done, bf16[3584,896]{1,0:T(8,128)(2,1)} %param.42), kind=kOutput, calls=%fused_computation.325 | convolution fusion | flops 1644167168 | bytes 9175040 | tf_op jit(solution)/shard_map/dot_general | solution.py:226
  440.0 56.4 %while.2 = (s32[]{:T(128)}, bf16[4,256,224]{1,2,0:T(8,128)(2,1)}, s32[4]{0:T(128)S(1)}, bf16[256,896]{1,0:T(8,128)(2,1)S(1)}, bf16[7424,896]{1,0:T(8,128)(2,1)},...) while((s32[]{:T(128)}, bf16[4,256,224]{1,2,0:T(8,128)(2,1)}, ...), condition=%wide.region_30.31_spmd, body=%wide.region_27.30_spmd.sunk | while | flops 1718148608 | bytes 32561836 | solution.py:279
  441.5 5.3 %fusion.116 = (f32[256]{0:T(256)S(1)}, f32[256,7424]{1,0:T(8,128)S(1)}) fusion(pred[256,7424]{1,0:T(32,128)(4,1)S(1)} %get-tuple-element.372, bf16[7424,896]{1,0:T(8,128)(2,1)} %get-tuple-element.371, s32[]{:T(128)S(6)} %select_n.229, bf16[256,896]{1,0:T(8,128)(2,1)S(1)} %get-tuple-element.370), kind=kOutput, calls=%fused_computation.322.clone.1 | convolution fusion | flops 857145088 | bytes 13436928 | tf_op jit(solution)/shard_map/while/body/eval_jaxpr/dot_general | solution.py:268
  448.0 6.6 %fusion.118 = bf16[4,256,224]{1,2,0:T(8,128)(2,1)} fusion(bf16[4,256,224]{1,2,0:T(8,128)(2,1)} %get-tuple-element.357, s32[]{:T(128)} %get-tuple-element.356, bf16[7424,896]{1,0:T(8,128)(2,1)} %get-tuple-element.373, s32[]{:T(128)S(6)} %select_n.229, f32[256,7424]{1,0:T(8,128)S(1)} %get-tuple-element.343, f32[256]{0:T(256)S(1)} %fusion.117, ...), kind=kOutput, calls=%fused_computation.11.clone.1 | convolution fusion | flops 857202688 | bytes 11520516 | tf_op jit(solution)/shard_map/while/body/eval_jaxpr/dot_general | solution.py:277
  455.8 5.3 %fusion.116 = (f32[256]{0:T(256)S(1)}, f32[256,7424]{1,0:T(8,128)S(1)}) fusion(pred[256,7424]{1,0:T(32,128)(4,1)S(1)} %get-tuple-element.372, bf16[7424,896]{1,0:T(8,128)(2,1)} %get-tuple-element.371, s32[]{:T(128)S(6)} %select_n.229, bf16[256,896]{1,0:T(8,128)(2,1)S(1)} %get-tuple-element.370), kind=kOutput, calls=%fused_computation.322.clone.1 | convolution fusion | flops 857145088 | bytes 13436928 | tf_op jit(solution)/shard_map/while/body/eval_jaxpr/dot_general | solution.py:268
  462.3 6.6 %fusion.118 = bf16[4,256,224]{1,2,0:T(8,128)(2,1)} fusion(bf16[4,256,224]{1,2,0:T(8,128)(2,1)} %get-tuple-element.357, s32[]{:T(128)} %get-tuple-element.356, bf16[7424,896]{1,0:T(8,128)(2,1)} %get-tuple-element.373, s32[]{:T(128)S(6)} %select_n.229, f32[256,7424]{1,0:T(8,128)S(1)} %get-tuple-element.343, f32[256]{0:T(256)S(1)} %fusion.117, ...), kind=kOutput, calls=%fused_computation.11.clone.1 | convolution fusion | flops 857202688 | bytes 11520516 | tf_op jit(solution)/shard_map/while/body/eval_jaxpr/dot_general | solution.py:277
  470.2 5.3 %fusion.116 = (f32[256]{0:T(256)S(1)}, f32[256,7424]{1,0:T(8,128)S(1)}) fusion(pred[256,7424]{1,0:T(32,128)(4,1)S(1)} %get-tuple-element.372, bf16[7424,896]{1,0:T(8,128)(2,1)} %get-tuple-element.371, s32[]{:T(128)S(6)} %select_n.229, bf16[256,896]{1,0:T(8,128)(2,1)S(1)} %get-tuple-element.370), kind=kOutput, calls=%fused_computation.322.clone.1 | convolution fusion | flops 857145088 | bytes 13436928 | tf_op jit(solution)/shard_map/while/body/eval_jaxpr/dot_general | solution.py:268
  476.7 6.6 %fusion.118 = bf16[4,256,224]{1,2,0:T(8,128)(2,1)} fusion(bf16[4,256,224]{1,2,0:T(8,128)(2,1)} %get-tuple-element.357, s32[]{:T(128)} %get-tuple-element.356, bf16[7424,896]{1,0:T(8,128)(2,1)} %get-tuple-element.373, s32[]{:T(128)S(6)} %select_n.229, f32[256,7424]{1,0:T(8,128)S(1)} %get-tuple-element.343, f32[256]{0:T(256)S(1)} %fusion.117, ...), kind=kOutput, calls=%fused_computation.11.clone.1 | convolution fusion | flops 857202688 | bytes 11520516 | tf_op jit(solution)/shard_map/while/body/eval_jaxpr/dot_general | solution.py:277
  484.5 4.7 fusion.116
  490.4 6.0 %fusion.118 = bf16[4,256,224]{1,2,0:T(8,128)(2,1)} fusion(bf16[4,256,224]{1,2,0:T(8,128)(2,1)} %get-tuple-element.357, s32[]{:T(128)} %get-tuple-element.356, bf16[7424,896]{1,0:T(8,128)(2,1)} %get-tuple-element.373, s32[]{:T(128)S(6)} %select_n.229, f32[256,7424]{1,0:T(8,128)S(1)} %get-tuple-element.343, f32[256]{0:T(256)S(1)} %fusion.117, ...), kind=kOutput, calls=%fused_computation.11.clone.1 | convolution fusion | flops 857202688 | bytes 11520516 | tf_op jit(solution)/shard_map/while/body/eval_jaxpr/dot_general | solution.py:277
  (288 shorter events, 184.2 us)
Async XLA Ops:
  7.2 430.2 %copy-start = (bf16[3584,128]{1,0:T(8,128)(2,1)S(1)}, bf16[3584,128]{1,0:T(8,128)(2,1)}, u32[]{:S(2)}) copy-start(bf16[3584,128]{1,0:T(8,128)(2,1)} %param.43) | copy-start | bytes 2752516
  7.2 392.0 %reduce-scatter.2.cloned.1.call-start = ((), (), s32[]{:S(2)}) async-start(), calls=%async_computation.1 | async-start | bytes 4587520 | tf_op jit(solution)/shard_map/reduce_scatter | solution.py:212
  10.3 43.4 %collective-permute-start = (bf16[4,256,896]{2,1,0:T(8,128)(2,1)}, bf16[4,256,896]{2,1,0:T(8,128)(2,1)}, u32[]{:S(2)}, u32[]{:S(2)}) collective-permute-start(bf16[4,256,896]{2,1,0:T(8,128)(2,1)} %pad_maximum_fusion), channel_id=1, source_target_pairs={{0,4},{4,8},{8,12},{12,16},{16,20},{20,24},{24,28},{28,32},{32,36}... | collective-permute-start | bytes 5505032 | tf_op jit(solution)/shard_map/ppermute | solution.py:16
  15.2 42.3 %collective-permute-start.2 = (bf16[4,256,896]{2,1,0:T(8,128)(2,1)}, bf16[4,256,896]{2,1,0:T(8,128)(2,1)S(1)}, u32[]{:S(2)}, u32[]{:S(2)}) collective-permute-start(bf16[4,256,896]{2,1,0:T(8,128)(2,1)} %pad_maximum_fusion), channel_id=1, source_target_pairs={{0,32},{4,36},{8,40},{12,44},{16,48},{20,52},{24,56},{28,60},{32,6... | collective-permute-start | bytes 5505032 | tf_op jit(solution)/shard_map/ppermute | solution.py:16
  20.8 32.9 %collective-permute-start.1 = (bf16[2,256,896]{2,1,0:T(8,128)(2,1)}, bf16[2,256,896]{2,1,0:T(8,128)(2,1)}, u32[]{:S(2)}, u32[]{:S(2)}) collective-permute-start(bf16[2,256,896]{2,1,0:T(8,128)(2,1)} %pad_maximum_fusion.1), channel_id=1, source_target_pairs={{4,0},{8,4},{12,8},{16,12},{20,16},{24,20},{28,24},{32,28},{36,32}... | collective-permute-start | bytes 2752520 | tf_op jit(solution)/shard_map/ppermute | solution.py:16
  22.7 31.0 %collective-permute-start.3 = (bf16[2,256,896]{2,1,0:T(8,128)(2,1)}, bf16[2,256,896]{2,1,0:T(8,128)(2,1)}, u32[]{:S(2)}, u32[]{:S(2)}) collective-permute-start(bf16[2,256,896]{2,1,0:T(8,128)(2,1)} %pad_maximum_fusion.1), channel_id=1, source_target_pairs={{32,0},{36,4},{40,8},{44,12},{48,16},{52,20},{56,24},{60,28},{64,3... | collective-permute-start | bytes 2752520 | tf_op jit(solution)/shard_map/ppermute | solution.py:16
  25.2 20.0 %collective-permute-start.5 = (bf16[3,128]{1,0:T(4,128)(2,1)}, bf16[3,128]{1,0:T(4,128)(2,1)}, u32[]{:S(2)}, u32[]{:S(2)}) collective-permute-start(bf16[3,128]{1,0:T(4,128)(2,1)} %slice.304), channel_id=1, source_target_pairs={{0,4},{4,8},{8,12},{12,16},{16,20},{20,24},{24,28},{28,32},{32,36}... | collective-permute-start | bytes 2312 | tf_op jit(solution)/shard_map/ppermute | solution.py:16
  45.3 4.0 collective-permute-start.4
  57.5 67.5 %collective-permute-start.6 = (bf16[4,256,896]{2,1,0:T(8,128)(2,1)}, bf16[4,256,896]{2,1,0:T(8,128)(2,1)}, u32[]{:S(2)}, u32[]{:S(2)}) collective-permute-start(bf16[4,256,896]{2,1,0:T(8,128)(2,1)} %collective-permute-done), channel_id=1, source_target_pairs={{0,4},{4,8},{8,12},{12,16},{16,20},{20,24},{24,28},{28,32},{32,36}... | collective-permute-start | bytes 5505032 | tf_op jit(solution)/shard_map/ppermute | solution.py:16
  60.3 65.0 %collective-permute-start.8 = (bf16[4,256,896]{2,1,0:T(8,128)(2,1)}, bf16[4,256,896]{2,1,0:T(8,128)(2,1)}, u32[]{:S(2)}, u32[]{:S(2)}) collective-permute-start(bf16[4,256,896]{2,1,0:T(8,128)(2,1)} %collective-permute-done), channel_id=1, source_target_pairs={{0,32},{4,36},{8,40},{12,44},{16,48},{20,52},{24,56},{28,60},{32,6... | collective-permute-start | bytes 5505032 | tf_op jit(solution)/shard_map/ppermute | solution.py:16
  95.7 15.0 %collective-permute-start.7 = (bf16[2,256,896]{2,1,0:T(8,128)(2,1)}, bf16[2,256,896]{2,1,0:T(8,128)(2,1)}, u32[]{:S(2)}, u32[]{:S(2)}) collective-permute-start(bf16[2,256,896]{2,1,0:T(8,128)(2,1)} %collective-permute-done.1), channel_id=1, source_target_pairs={{4,0},{8,4},{12,8},{16,12},{20,16},{24,20},{28,24},{32,28},{36,32}... | collective-permute-start | bytes 2752520 | tf_op jit(solution)/shard_map/ppermute | solution.py:16
  102.4 22.6 %collective-permute-start.9 = (bf16[2,256,896]{2,1,0:T(8,128)(2,1)}, bf16[2,256,896]{2,1,0:T(8,128)(2,1)}, u32[]{:S(2)}, u32[]{:S(2)}) collective-permute-start(bf16[2,256,896]{2,1,0:T(8,128)(2,1)} %collective-permute-done.1), channel_id=1, source_target_pairs={{32,0},{36,4},{40,8},{44,12},{48,16},{52,20},{56,24},{60,28},{64,3... | collective-permute-start | bytes 2752520 | tf_op jit(solution)/shard_map/ppermute | solution.py:16
  125.3 27.4 %collective-permute-start.10 = (bf16[4,256,896]{2,1,0:T(8,128)(2,1)}, bf16[4,256,896]{2,1,0:T(8,128)(2,1)S(1)}, u32[]{:S(2)}, u32[]{:S(2)}) collective-permute-start(bf16[4,256,896]{2,1,0:T(8,128)(2,1)} %collective-permute-done.6), channel_id=1, source_target_pairs={{0,4},{4,8},{8,12},{12,16},{16,20},{20,24},{24,28},{28,32},{32,36}... | collective-permute-start | bytes 5505032 | tf_op jit(solution)/shard_map/ppermute | solution.py:16
  128.4 24.3 %collective-permute-start.11 = (bf16[2,256,896]{2,1,0:T(8,128)(2,1)}, bf16[2,256,896]{2,1,0:T(8,128)(2,1)S(1)}, u32[]{:S(2)}, u32[]{:S(2)}) collective-permute-start(bf16[2,256,896]{2,1,0:T(8,128)(2,1)} %collective-permute-done.7), channel_id=1, source_target_pairs={{4,0},{8,4},{12,8},{16,12},{20,16},{24,20},{28,24},{32,28},{36,32}... | collective-permute-start | bytes 2752520 | tf_op jit(solution)/shard_map/ppermute | solution.py:16
  141.8 10.8 %collective-permute-start.13 = (f32[14,64,64]{2,1,0:T(8,128)S(1)}, f32[14,64,64]{2,1,0:T(8,128)S(1)}, u32[]{:S(2)}, u32[]{:S(2)}) collective-permute-start(f32[14,64,64]{2,1,0:T(8,128)S(1)} %convolution_add_fusion.1), channel_id=1, source_target_pairs={{0,4},{4,8},{8,12},{12,16},{16,20},{20,24},{24,28},{28,32},{32,36}... | collective-permute-start | bytes 688136 | tf_op jit(solution)/shard_map/ppermute | solution.py:16
  143.8 8.8 %collective-permute-start.12 = (f32[14]{0:T(128)S(1)}, f32[14]{0:T(128)S(1)}, u32[]{:S(2)}, u32[]{:S(2)}) collective-permute-start(f32[14]{0:T(128)S(1)} %get-tuple-element.99), channel_id=1, source_target_pairs={{0,4},{4,8},{8,12},{12,16},{16,20},{20,24},{24,28},{28,32},{32,36}... | collective-permute-start | bytes 176 | tf_op jit(solution)/shard_map/ppermute | solution.py:16
  152.7 126.7 %copy-start.8 = (bf16[4,256,896]{2,1,0:T(8,128)(2,1)}, bf16[4,256,896]{2,1,0:T(8,128)(2,1)S(1)}, u32[]{:S(2)}) copy-start(bf16[4,256,896]{2,1,0:T(8,128)(2,1)S(1)} %collective-permute-done.10) | copy-start | bytes 5505028
  152.7 34.6 %collective-permute-start.14 = (bf16[4,256,896]{2,1,0:T(8,128)(2,1)S(1)}, bf16[4,256,896]{2,1,0:T(8,128)(2,1)S(1)}, u32[]{:S(2)}, u32[]{:S(2)}) collective-permute-start(bf16[4,256,896]{2,1,0:T(8,128)(2,1)S(1)} %collective-permute-done.10), channel_id=1, source_target_pairs={{0,4},{4,8},{8,12},{12,16},{16,20},{20,24},{24,28},{28,32},{32,36}... | collective-permute-start | bytes 5505032 | tf_op jit(solution)/shard_map/ppermute | solution.py:16
  158.3 29.0 %collective-permute-start.15 = (bf16[2,256,896]{2,1,0:T(8,128)(2,1)S(1)}, bf16[2,256,896]{2,1,0:T(8,128)(2,1)S(1)}, u32[]{:S(2)}, u32[]{:S(2)}) collective-permute-start(bf16[2,256,896]{2,1,0:T(8,128)(2,1)S(1)} %collective-permute-done.11), channel_id=1, source_target_pairs={{4,0},{8,4},{12,8},{16,12},{20,16},{24,20},{28,24},{32,28},{36,32}... | collective-permute-start | bytes 2752520 | tf_op jit(solution)/shard_map/ppermute | solution.py:16
  160.3 26.9 %collective-permute-start.17 = (f32[14,64,64]{2,1,0:T(8,128)S(1)}, f32[14,64,64]{2,1,0:T(8,128)S(1)}, u32[]{:S(2)}, u32[]{:S(2)}) collective-permute-start(f32[14,64,64]{2,1,0:T(8,128)S(1)} %multiply_add_fusion.3), channel_id=1, source_target_pairs={{0,8},{4,12},{8,16},{12,20},{16,24},{20,28},{24,32},{28,36},{32,40... | collective-permute-start | bytes 688136 | tf_op jit(solution)/shard_map/ppermute | solution.py:16
  173.5 13.7 %collective-permute-start.16 = (f32[14]{0:T(128)S(1)}, f32[14]{0:T(128)S(1)}, u32[]{:S(2)}, u32[]{:S(2)}) collective-permute-start(f32[14]{0:T(128)S(1)} %mul.385), channel_id=1, source_target_pairs={{0,8},{4,12},{8,16},{12,20},{16,24},{20,28},{24,32},{28,36},{32,40... | collective-permute-start | bytes 176 | tf_op jit(solution)/shard_map/ppermute | solution.py:16
  187.4 46.9 %collective-permute-start.18 = (bf16[4,256,896]{2,1,0:T(8,128)(2,1)S(1)}, bf16[4,256,896]{2,1,0:T(8,128)(2,1)S(1)}, u32[]{:S(2)}, u32[]{:S(2)}) collective-permute-start(bf16[4,256,896]{2,1,0:T(8,128)(2,1)S(1)} %collective-permute-done.14), channel_id=1, source_target_pairs={{0,4},{4,8},{8,12},{12,16},{16,20},{20,24},{24,28},{28,32},{32,36}... | collective-permute-start | bytes 5505032 | tf_op jit(solution)/shard_map/ppermute | solution.py:16
  197.5 36.8 %collective-permute-start.19 = (bf16[2,256,896]{2,1,0:T(8,128)(2,1)S(1)}, bf16[2,256,896]{2,1,0:T(8,128)(2,1)S(1)}, u32[]{:S(2)}, u32[]{:S(2)}) collective-permute-start(bf16[2,256,896]{2,1,0:T(8,128)(2,1)S(1)} %collective-permute-done.15), channel_id=1, source_target_pairs={{4,0},{8,4},{12,8},{16,12},{20,16},{24,20},{28,24},{32,28},{36,32}... | collective-permute-start | bytes 2752520 | tf_op jit(solution)/shard_map/ppermute | solution.py:16
  199.6 34.6 %collective-permute-start.21 = (f32[14,64,64]{2,1,0:T(8,128)S(1)}, f32[14,64,64]{2,1,0:T(8,128)S(1)}, u32[]{:S(2)}, u32[]{:S(2)}) collective-permute-start(f32[14,64,64]{2,1,0:T(8,128)S(1)} %multiply_add_fusion.2), channel_id=1, source_target_pairs={{0,16},{4,20},{8,24},{12,28},{16,32},{20,36},{24,40},{28,44},{32,4... | collective-permute-start | bytes 688136 | tf_op jit(solution)/shard_map/ppermute | solution.py:16
  218.1 16.0 %collective-permute-start.20 = (f32[14]{0:T(128)S(1)}, f32[14]{0:T(128)S(1)}, u32[]{:S(2)}, u32[]{:S(2)}) collective-permute-start(f32[14]{0:T(128)S(1)} %mul.388), channel_id=1, source_target_pairs={{0,16},{4,20},{8,24},{12,28},{16,32},{20,36},{24,40},{28,44},{32,4... | collective-permute-start | bytes 176 | tf_op jit(solution)/shard_map/ppermute | solution.py:16
  234.3 34.5 %collective-permute-start.22 = (bf16[4,256,896]{2,1,0:T(8,128)(2,1)S(1)}, bf16[4,256,896]{2,1,0:T(8,128)(2,1)}, u32[]{:S(2)}, u32[]{:S(2)}) collective-permute-start(bf16[4,256,896]{2,1,0:T(8,128)(2,1)S(1)} %collective-permute-done.18), channel_id=1, source_target_pairs={{0,4},{4,8},{8,12},{12,16},{16,20},{20,24},{24,28},{28,32},{32,36}... | collective-permute-start | bytes 5505032 | tf_op jit(solution)/shard_map/ppermute | solution.py:16
  249.3 16.8 %collective-permute-start.23 = (bf16[2,256,896]{2,1,0:T(8,128)(2,1)S(1)}, bf16[2,256,896]{2,1,0:T(8,128)(2,1)}, u32[]{:S(2)}, u32[]{:S(2)}) collective-permute-start(bf16[2,256,896]{2,1,0:T(8,128)(2,1)S(1)} %collective-permute-done.19), channel_id=1, source_target_pairs={{4,0},{8,4},{12,8},{16,12},{20,16},{24,20},{28,24},{32,28},{36,32}... | collective-permute-start | bytes 2752520 | tf_op jit(solution)/shard_map/ppermute | solution.py:16
  251.4 13.9 %collective-permute-start.24 = (f32[14,64,64]{2,1,0:T(8,128)S(1)}, f32[14,64,64]{2,1,0:T(8,128)S(1)}, u32[]{:S(2)}, u32[]{:S(2)}) collective-permute-start(f32[14,64,64]{2,1,0:T(8,128)S(1)} %multiply_add_fusion.1), channel_id=1, source_target_pairs={{0,32},{4,36},{8,40},{12,44},{16,48},{20,52},{24,56},{28,60},{32,6... | collective-permute-start | bytes 688136 | tf_op jit(solution)/shard_map/ppermute | solution.py:16
  268.8 35.2 %collective-permute-start.25 = (bf16[4,256,896]{2,1,0:T(8,128)(2,1)}, bf16[4,256,896]{2,1,0:T(8,128)(2,1)}, u32[]{:S(2)}, u32[]{:S(2)}) collective-permute-start(bf16[4,256,896]{2,1,0:T(8,128)(2,1)} %collective-permute-done.22), channel_id=1, source_target_pairs={{0,4},{4,8},{8,12},{12,16},{16,20},{20,24},{24,28},{28,32},{32,36}... | collective-permute-start | bytes 5505032 | tf_op jit(solution)/shard_map/ppermute | solution.py:16
  279.4 24.5 %collective-permute-start.26 = (bf16[2,256,896]{2,1,0:T(8,128)(2,1)}, bf16[2,256,896]{2,1,0:T(8,128)(2,1)}, u32[]{:S(2)}, u32[]{:S(2)}) collective-permute-start(bf16[2,256,896]{2,1,0:T(8,128)(2,1)} %collective-permute-done.23), channel_id=1, source_target_pairs={{4,0},{8,4},{12,8},{16,12},{20,16},{24,20},{28,24},{32,28},{36,32}... | collective-permute-start | bytes 2752520 | tf_op jit(solution)/shard_map/ppermute | solution.py:16
  289.7 14.2 %collective-permute-start.27 = (f32[14,64,64]{2,1,0:T(8,128)S(1)}, f32[14,64,64]{2,1,0:T(8,128)S(1)}, u32[]{:S(2)}, u32[]{:S(2)}) collective-permute-start(f32[14,64,64]{2,1,0:T(8,128)S(1)} %copy-done.23), channel_id=1, source_target_pairs={{0,4},{4,8},{8,12},{12,16},{16,20},{20,24},{24,28},{28,32},{32,36}... | collective-permute-start | bytes 688136 | tf_op jit(solution)/shard_map/ppermute | solution.py:16
  343.5 87.5 %all-gather.2.cloned.1.call-start = ((), (), s32[]{:S(2)}) async-start(), calls=%async_computation.2 | async-start | bytes 2293760 | tf_op jit(solution)/shard_map/all_gather | solution.py:223
  (29 other events, 743.4 us)
Sparse Core Ops, SparseCore 0:
  343.6 55.5 reduce-scatter.1
  402.6 28.3 all-gather.1
